TPU v7x, 32 devices: a whole 2x2x4 slice. The times are simulated.
32 devices in a mesh: snode: 16 (over z, y, x), row: 2 (over core).
Axes of the slice: x: 2, y: 2, z: 4, core: 2. Of those that a mesh axis runs over, the one named last changes fastest.
Arguments:
- ancestor_sigma: bfloat16 [8192, 8192], P('row', 'snode'), may hold values from -8 to 8, as said below
- child_panels: bfloat16 [96, 4096, 128], P('snode', 'row'), may hold values from -1 to 1
- diagonal_inverse_blocks: float32 [96, 128, 128], P('snode', 'row'), may hold values from -4 to 4, as said below
- block_list: int32 [96, 32], P('snode'), may hold values from 0 to 63, as said below
- block_count: int32 [96], P('snode'), may hold values from 8 to 32, as said below
- child_width: int32 [96], P('snode'), may hold values from 64 to 128, as said below
- owner_slot: int32 [64], replicated, may hold values from 0 to 63, each once
Outputs:
- selected_panel_inverse: float32 [8192, 96, 128], P('row', 'snode')
- selected_diagonal_inverse: float32 [96, 128, 128], P('snode', 'row')
Inputs may be any that keep to these rules, and one draw needn't show every extreme that they name: `ancestor_sigma`: symmetric. `diagonal_inverse_blocks`: each child's block is symmetric. `block_list`: the 32 entries of a row are distinct and ascending. `block_count`: some child has exactly 32. `child_width`: some child has exactly 128.
All inputs are finite; a program needn't handle non-finite values.
Results may differ from a plain program's by a relative error of at most 0.0003.
Values may be sent and summed in bfloat16 or wider, within the bound.
No kernel may reach another device: no remote copies, remote signals or barrier semaphores. Data moves between devices by JAX's collectives and lax.ppermute only.
A program may use at most 192 MiB of HBM per device.

v0:
```python
import jax
import jax.numpy as jnp
from jax import lax
from jax.sharding import PartitionSpec as P

B = 128
KMAX = 32
WJ = 128
NB = 64


def slot_table(block_list, block_count, child_width, owner_slot):
    block_ids = jnp.arange(NB, dtype=jnp.int32)
    named = block_list[:, :, None] == block_ids[None, None, :]
    slot_ids = jnp.sum(jnp.where(named, owner_slot[None, None, :], 0), axis=2)
    valid_blocks = jnp.arange(KMAX, dtype=jnp.int32)[None, :] < block_count[:, None]
    placed = (slot_ids[:, :, None] == block_ids[None, None, :]) & valid_blocks[:, :, None]
    active_columns = jnp.arange(WJ, dtype=jnp.int32)[None, :] < child_width[:, None]
    return (placed, active_columns)


def expand_rows(place_table, blocks):
    children = blocks.shape[0]
    spread = jnp.einsum("ckn,ckbj->nbcj", place_table, blocks, preferred_element_type=jnp.float32)
    return spread.astype(jnp.bfloat16).reshape(place_table.shape[2] * B, children * WJ)


def body(
    ancestor_sigma,
    child_panels,
    diagonal_inverse_blocks,
    block_list,
    block_count,
    child_width,
    owner_slot,
):
    row_devices = lax.axis_size("row")
    row_positions = lax.axis_index("row")
    children = child_panels.shape[0]
    local_rows = ancestor_sigma.shape[0]
    placed, active_columns = slot_table(block_list, block_count, child_width, owner_slot)
    place_bf = placed.astype(jnp.bfloat16)
    gathered = lax.all_gather(child_panels, "row", axis=1, tiled=True)
    blocks = gathered.reshape(children, KMAX, B, WJ)
    blocks = jnp.where(active_columns[:, None, None, :], blocks, jnp.zeros_like(blocks))
    panel_rows = expand_rows(place_bf, blocks)
    product = jnp.dot(
        lax.all_gather(ancestor_sigma, "snode", axis=1, tiled=True),
        panel_rows,
        preferred_element_type=jnp.float32,
    )
    product_table = product.reshape(local_rows, children, WJ)
    own_blocks = local_rows // B
    own_table = lax.dynamic_slice_in_dim(place_bf, row_positions * own_blocks, own_blocks, 2)
    own_rows = expand_rows(own_table, blocks).reshape(local_rows, children, WJ).astype(jnp.float32)
    partial_value = jnp.einsum(
        "nca,ncb->cab", own_rows, product_table, precision=lax.Precision.HIGHEST
    )
    shared_rows = WJ // row_devices
    reduced_total = lax.psum(partial_value, "row")
    reduced_total = lax.dynamic_slice_in_dim(
        reduced_total, row_positions * shared_rows, shared_rows, 1
    )
    active_flags = active_columns.astype(jnp.float32)
    owned_active = lax.dynamic_slice_in_dim(
        active_flags, row_positions * shared_rows, shared_rows, 1
    )
    selected_diagonal_inverse = (
        (diagonal_inverse_blocks + reduced_total)
        * owned_active[:, :, None]
        * active_flags[:, None, :]
    )
    slot_live = jnp.sum(placed.astype(jnp.float32), axis=1)
    own_slots = lax.dynamic_slice_in_dim(slot_live, row_positions * own_blocks, own_blocks, 1)
    active_rows = jnp.repeat(own_slots.T, B, axis=0)
    selected_panel_inverse = -product_table * active_rows[:, :, None] * active_flags[None, :, :]
    return (selected_panel_inverse, selected_diagonal_inverse)


def solution(mesh):
    placed = (
        P("row", "snode"),
        P("snode", "row", None),
        P("snode", "row", None),
        P("snode", None),
        P("snode"),
        P("snode"),
        P(),
    )
    return jax.shard_map(
        body,
        mesh=mesh,
        in_specs=placed,
        out_specs=(P("row", "snode", None), P("snode", "row", None)),
        check_vma=False,
    )
```

profile of v0, /device:TPU:0, one launch (start us, length us, event | category | flops | bytes accessed | tf_op | source)
XLA Modules:
  0.0 926.9 jit_solution(1576795213915367664)
XLA Ops:
  7.2 0.7 all-gather.3.cloned.1.call-update
  7.9 0.0 all-gather.5.cloned.1.call-start
  7.9 0.7 all-gather.5.cloned.1.call-update
  8.6 0.0 all-reduce.2.cloned.1.call-start
  8.7 1.0 select_reduce_fusion
  9.7 0.7 iota_compare_fusion.2
  10.4 0.1 convert_reduce_fusion
  10.5 0.1 dynamic-slice_bitcast_fusion
  10.6 0.1 broadcast_bitcast_fusion
  10.7 0.1 copy.45
  10.8 0.7 fusion.13
  11.5 0.1 constant_dynamic-slice_fusion
  11.6 17.4 %all-gather.3.cloned.1.call-done = bf16[6,4096,128]{2,1,0:T(8,128)(2,1)} async-done(((bf16[6,2048,128]{2,1,0:T(8,128)(2,1)}), bf16[6,4096,128]{2,1,0:T(8,128)(2,1)}) %all-gather.3.cloned.1.call-update) | async-done | bytes 6291472 | tf_op jit(solution)/shard_map/all_gather | solution.py:43
  29.0 7.3 convert_bitcast_fusion.1
  36.3 5.7 copy.24
  42.0 7.3 convert_bitcast_fusion
  49.3 18.1 %copy.22 = bf16[64,128,6,128]{1,0,3,2:T(8,128)(2,1)} copy(bf16[64,128,6,128]{3,0,1,2:T(8,128)(2,1)} %convert_bitcast_fusion) | data formatting | bytes 25165824 | tf_op jit(solution)/shard_map/convert_element_type | solution.py:25
  67.4 690.1 %all-gather.5.cloned.1.call-done = bf16[4096,8192]{1,0:T(8,128)(2,1)} async-done(((bf16[4096,512]{1,0:T(8,128)(2,1)}), bf16[4096,8192]{1,0:T(8,128)(2,1)}) %all-gather.5.cloned.1.call-update) | async-done | bytes 67108880 | tf_op jit(solution)/shard_map/all_gather | solution.py:48
  757.6 117.5 %fusion = f32[768,4096]{1,0:T(8,128)} fusion(bf16[4096,8192]{1,0:T(8,128)(2,1)} %all-gather.5.cloned.1.call-done, bf16[96,8,64,128]{3,2,1,0:T(8,128)(2,1)} %bitcast.41), kind=kOutput, calls=%fused_computation | convolution fusion | flops 51539607552 | bytes 92274688 | tf_op jit(solution)/shard_map/dot_general | solution.py:47
  875.1 12.6 %copy.23 = f32[4096,6,128]{2,0,1:T(8,128)} copy(f32[4096,6,128]{0,2,1:T(8,128)} %bitcast.38) | data formatting | bytes 25165824 | tf_op jit(solution)/shard_map/reshape | solution.py:52
  887.7 14.1 %fusion.15 = f32[6,128,128]{2,1,0:T(8,128)} fusion(bf16[4096,6,128]{2,0,1:T(8,128)(2,1)} %bitcast.40, f32[4096,6,128]{0,2,1:T(8,128)} %bitcast.39), kind=kOutput, calls=%fused_computation.29 | convolution fusion | flops 4831838208 | bytes 19267584 | tf_op jit(solution)/shard_map/nca,ncb->cab/dot_general | solution.py:56
  901.8 11.7 %multiply_multiply_fusion = f32[4096,6,128]{2,0,1:T(8,128)} fusion(f32[4096,6,128]{2,0,1:T(8,128)} %copy.23, f32[6,128]{1,0:T(8,128)S(1)} %get-tuple-element.2, f32[4096,6]{0,1:T(8,128)S(1)} %bitcast.46), kind=kLoop, calls=%fused_computation.3 | loop fusion | flops 9437184 | bytes 25267200 | tf_op jit(solution)/shard_map/mul | solution.py:76
  913.5 5.1 all-reduce.2.cloned.1.call-done
  918.6 1.7 multiply_multiply_fusion.1
  (10 shorter events, 0.1 us)
Async XLA Ops:
  7.2 21.9 %all-gather.3.cloned.1.call-start = ((), (), s32[]{:S(2)}) async-start(), calls=%async_computation | async-start | bytes 9437184 | tf_op jit(solution)/shard_map/all_gather | solution.py:43
  7.9 749.7 %all-gather.5.cloned.1.call-start = ((), (), s32[]{:S(2)}) async-start(), calls=%async_computation.1 | async-start | bytes 71303168 | tf_op jit(solution)/shard_map/all_gather | solution.py:48
  8.6 910.0 %all-reduce.2.cloned.1.call-start = ((), (), s32[]{:S(2)}) async-start(), calls=%async_computation.2 | async-start | bytes 786432 | tf_op jit(solution)/shard_map/psum | solution.py:60
  29.0 13.0 %slice-start = ((s8[6291456]{0:T(1024)(128)(4,1)}), s8[4194304]{0:T(1024)(128)(4,1)S(1)}, s32[]{:S(2)}) async-start(s8[6291456]{0:T(1024)(128)(4,1)} %bitcast.43), calls=%async_computation.3 | async-start | bytes 8388608
  29.0 13.0 %slice-start.1 = ((s8[6291456]{0:T(1024)(128)(4,1)}), s8[2097152]{0:T(1024)(128)(4,1)S(1)}, s32[]{:S(2)}) async-start(s8[6291456]{0:T(1024)(128)(4,1)} %bitcast.43), calls=%async_computation.4 | async-start | bytes 4194304
  901.8 16.8 %copy-start = (f32[6,64,128]{2,1,0:T(8,128)S(1)}, f32[6,64,128]{2,1,0:T(8,128)}, u32[]{:S(2)}) copy-start(f32[6,64,128]{2,1,0:T(8,128)} %param.9) | copy-start | bytes 589828
Sparse Core Ops, SparseCore 0:
  9.5 19.4 all-gather.2
  31.8 725.7 all-gather.4
  901.9 16.6 all-reduce.1
where the time goes:
time: 928 us; the launch traced here: 927 us
  waiting for transfers between devices  714 us (77%)
  matrix products  146 us (16%)
  local copies, waits for them, and re-layouts  36.7 us (4%)
  other arithmetic  16 us (2%)
  between operations  13.8 us (1%)
    all_gather x1, waiting for transfers between devices, body(): lax.all_gather(ancestor_sigma, 'snode', axis=1, tiled=True)  690 us
    dot_general x1, matrix products, body(): jnp.dot(lax.all_gather(ancestor_sigma, 'snode', axis=1, tiled=True), pane...  118 us
    convert_element_type x2, local copies, waits for them, and re-layouts, expand_rows(): spread.astype(jnp.bfloat16).reshape(place_table.shape[2] * B, children * WJ)  23.8 us
  transfers between devices with their start and end apart: 3, of which 3 were waited for; matrix products, arithmetic and copies ran while one was open for 6% of the time, Pallas kernels for 0%

commit v1 on v0

--- a/solution.py
+++ b/solution.py
@@ -1,12 +1,15 @@
+import numpy as np
 import jax
 import jax.numpy as jnp
 from jax import lax
+from jax.sharding import Mesh
 from jax.sharding import PartitionSpec as P
 
 B = 128
 KMAX = 32
 WJ = 128
 NB = 64
+GATHER_CHUNKS = 4
 
 
 def slot_table(block_list, block_count, child_width, owner_slot):
@@ -25,6 +28,12 @@
     return spread.astype(jnp.bfloat16).reshape(place_table.shape[2] * B, children * WJ)
 
 
+def masked_blocks(panels, active_columns):
+    children = panels.shape[0]
+    blocks = panels.reshape(children, KMAX, B, WJ)
+    return jnp.where(active_columns[:, None, None, :], blocks, jnp.zeros_like(blocks))
+
+
 def body(
     ancestor_sigma,
     child_panels,
@@ -35,21 +44,41 @@
     owner_slot,
 ):
     row_devices = lax.axis_size("row")
+    outer = lax.axis_size("so")
     row_positions = lax.axis_index("row")
     children = child_panels.shape[0]
     local_rows = ancestor_sigma.shape[0]
+    swap = [(y * row_devices + x, x * row_devices + y) for x in range(row_devices) for y in range(outer)]
+
+    own_panels = lax.all_gather(child_panels, "row", axis=1, tiled=True)
+    far_panels = lax.ppermute(own_panels, ("so", "row"), swap)
+    far_tables = lax.ppermute(
+        jnp.concatenate([block_list, block_count[:, None], child_width[:, None]], axis=1),
+        ("so", "row"),
+        swap,
+    )
+    far_placed, far_active = slot_table(
+        far_tables[:, :KMAX], far_tables[:, KMAX], far_tables[:, KMAX + 1], owner_slot
+    )
+    far_rows = expand_rows(far_placed.astype(jnp.bfloat16), masked_blocks(far_panels, far_active))
+
+    chunk = local_rows // GATHER_CHUNKS
+    far_rows = far_rows.reshape(row_devices, GATHER_CHUNKS, chunk, children * WJ)
+    product = None
+    for q in range(GATHER_CHUNKS):
+        piece = lax.all_gather(ancestor_sigma[q * chunk : (q + 1) * chunk], "si", axis=1, tiled=True)
+        piece = lax.all_gather(piece, "row", axis=0, tiled=True)
+        rows_q = far_rows[:, q].reshape(row_devices * chunk, children * WJ)
+        part = lax.dot_general(
+            piece, rows_q, (((0,), (0,)), ((), ())), preferred_element_type=jnp.float32
+        )
+        product = part if product is None else product + part
+    product = lax.ppermute(product, ("so", "row"), swap)
+    product_table = product.reshape(local_rows, children, WJ)
+
     placed, active_columns = slot_table(block_list, block_count, child_width, owner_slot)
     place_bf = placed.astype(jnp.bfloat16)
-    gathered = lax.all_gather(child_panels, "row", axis=1, tiled=True)
-    blocks = gathered.reshape(children, KMAX, B, WJ)
-    blocks = jnp.where(active_columns[:, None, None, :], blocks, jnp.zeros_like(blocks))
-    panel_rows = expand_rows(place_bf, blocks)
-    product = jnp.dot(
-        lax.all_gather(ancestor_sigma, "snode", axis=1, tiled=True),
-        panel_rows,
-        preferred_element_type=jnp.float32,
-    )
-    product_table = product.reshape(local_rows, children, WJ)
+    blocks = masked_blocks(own_panels, active_columns)
     own_blocks = local_rows // B
     own_table = lax.dynamic_slice_in_dim(place_bf, row_positions * own_blocks, own_blocks, 2)
     own_rows = expand_rows(own_table, blocks).reshape(local_rows, children, WJ).astype(jnp.float32)
@@ -78,19 +107,25 @@
 
 
 def solution(mesh):
+    snodes = mesh.shape["snode"]
+    rows = mesh.shape["row"]
+    grid = Mesh(
+        np.asarray(mesh.devices).reshape(rows, snodes // rows, rows), ("so", "si", "row")
+    )
+    sn = ("so", "si")
     placed = (
-        P("row", "snode"),
-        P("snode", "row", None),
-        P("snode", "row", None),
-        P("snode", None),
-        P("snode"),
-        P("snode"),
+        P("row", sn),
+        P(sn, "row", None),
+        P(sn, "row", None),
+        P(sn, None),
+        P(sn),
+        P(sn),
         P(),
     )
     return jax.shard_map(
         body,
-        mesh=mesh,
+        mesh=grid,
         in_specs=placed,
-        out_specs=(P("row", "snode", None), P("snode", "row", None)),
+        out_specs=(P("row", sn, None), P(sn, "row", None)),
         check_vma=False,
     )

time: 928 us -> 1310 us (1.41); the launches traced: 927 us -> 1290 us
  starting transfers between devices: 0.11 us -> 145 us
  local copies, waits for them, and re-layouts: 36.7 us -> 161 us
  waiting for transfers between devices: 714 us -> 833 us
  matrix products: 146 us -> 126 us
    psum x1, waiting for transfers between devices: 5.09 us -> 178 us  [body(): reduced_total = lax.psum(partial_value, 'row')]
    ppermute x0 -> x3, starting transfers between devices: none -> 145 us  [the longest x1 95.8 us: body(): product = lax.ppermute(product, ('so', 'row'), swap)]
    slice x0 -> x7, local copies, waits for them, and re-layouts: none -> 105 us  [the longest x5 101 us: body(): rows_q = far_rows[:, q].reshape(row_devices * chunk, children * WJ)]
    all_gather x2 -> x9, waiting for transfers between devices: 708 us -> 652 us  [the longest x4 629 us: body(): lax.all_gather(ancestor_sigma[q * chunk:(q + 1) * chunk], 'si', axis=1, t...]
    dot_general x1 -> x4, matrix products: 118 us -> 90.8 us  [body(): lax.dot_general(piece, rows_q, (((0,), (0,)), ((), ())), preferred_elemen...]
    another operation x0 -> x1, local copies, waits for them, and re-layouts: none -> 19.1 us  [body(): far_rows.reshape(row_devices, GATHER_CHUNKS, chunk, children * WJ)]
  transfers between devices with their start and end apart: 3 -> 13, of which waited for: 3 -> 6; matrix products, arithmetic and copies ran while one was open for 6% -> 19% of each run, Pallas kernels for 0% -> 0%
where the time goes in v1:
time: 1310 us; the launch traced here: 1290 us
  waiting for transfers between devices  833 us (64%)
  local copies, waits for them, and re-layouts  161 us (12%)
  starting transfers between devices  145 us (11%)
  matrix products  126 us (10%)
  between operations  14.5 us (1%)
  other arithmetic  14.3 us (1%)
    all_gather x4, waiting for transfers between devices, body(): lax.all_gather(ancestor_sigma[q * chunk:(q + 1) * chunk], 'si', axis=1, t...  629 us
    psum x1, waiting for transfers between devices, body(): reduced_total = lax.psum(partial_value, 'row')  178 us
    slice x5, local copies, waits for them, and re-layouts, body(): rows_q = far_rows[:, q].reshape(row_devices * chunk, children * WJ)  101 us
    ppermute x1, starting transfers between devices, body(): product = lax.ppermute(product, ('so', 'row'), swap)  95.8 us
    dot_general x4, matrix products, body(): lax.dot_general(piece, rows_q, (((0,), (0,)), ((), ())), preferred_elemen...  90.8 us
    ppermute x1, starting transfers between devices, body(): far_panels = lax.ppermute(own_panels, ('so', 'row'), swap)  48.6 us
  transfers between devices with their start and end apart: 13, of which 6 were waited for; matrix products, arithmetic and copies ran while one was open for 19% of the time, Pallas kernels for 0%

profile of v1, /device:TPU:0, one launch (start us, length us, event | category | flops | bytes accessed | tf_op | source)
XLA Modules:
  0.0 1294.0 jit_solution(4011462441385965458)
XLA Ops:
  14.2 166.0 %all-gather.12.cloned.1.call-done = bf16[1024,4096]{1,0:T(8,128)(2,1)} async-done(((bf16[1024,512]{1,0:T(8,128)(2,1)}), bf16[1024,4096]{1,0:T(8,128)(2,1)}) %all-gather.12.cloned.1.call-update) | async-done | bytes 8388624 | tf_op jit(solution)/shard_map/all_gather | solution.py:69
  180.3 171.5 %all-gather.16.cloned.1.call-done = bf16[1024,4096]{1,0:T(8,128)(2,1)} async-done(((bf16[1024,512]{1,0:T(8,128)(2,1)}), bf16[1024,4096]{1,0:T(8,128)(2,1)}) %all-gather.16.cloned.1.call-update) | async-done | bytes 8388624 | tf_op jit(solution)/shard_map/all_gather | solution.py:69
  351.8 171.5 %all-gather.20.cloned.1.call-done = bf16[1024,4096]{1,0:T(8,128)(2,1)} async-done(((bf16[1024,512]{1,0:T(8,128)(2,1)}), bf16[1024,4096]{1,0:T(8,128)(2,1)}) %all-gather.20.cloned.1.call-update) | async-done | bytes 8388624 | tf_op jit(solution)/shard_map/all_gather | solution.py:69
  523.4 22.3 %all-gather.10.cloned.1.call-done = bf16[6,4096,128]{2,1,0:T(8,128)(2,1)} async-done(((bf16[6,2048,128]{2,1,0:T(8,128)(2,1)}), bf16[6,4096,128]{2,1,0:T(8,128)(2,1)}) %all-gather.10.cloned.1.call-update) | async-done | bytes 6291472 | tf_op jit(solution)/shard_map/all_gather | solution.py:53
  545.7 48.6 %collective-permute-start.1 = (bf16[6,4096,128]{2,1,0:T(8,128)(2,1)}, bf16[6,4096,128]{2,1,0:T(8,128)(2,1)}, u32[]{:S(2)}, u32[]{:S(2)}) collective-permute-start(bf16[6,4096,128]{2,1,0:T(8,128)(2,1)} %all-gather.10.cloned.1.call-done), channel_id=1, source_target_pairs={{0,0},{16,1},{1,16},{17,17},{2,2},{18,3},{3,18},{19,19},{4,4},{20,... | collective-permute-start | bytes 18874376 | tf_op jit(solution)/shard_map/ppermute | solution.py:54
  594.2 120.4 %all-gather.24.cloned.1.call-done = bf16[1024,4096]{1,0:T(8,128)(2,1)} async-done(((bf16[1024,512]{1,0:T(8,128)(2,1)}), bf16[1024,4096]{1,0:T(8,128)(2,1)}) %all-gather.24.cloned.1.call-update) | async-done | bytes 8388624 | tf_op jit(solution)/shard_map/all_gather | solution.py:69
  716.5 13.8 %convert_bitcast_fusion = bf16[64,128,6,128]{3,0,1,2:T(8,128)(2,1)} fusion(bf16[6,32,128,128]{3,2,1,0:T(8,128)(2,1)} %bitcast.2, pred[6,128]{1,0:T(8,128)(4,1)S(1)} %iota_compare_fusion.7, s32[6,32]{1,0:T(8,128)S(1)} %get-tuple-element.5, pred[6,32]{1,0:T(8,128)(4,1)S(1)} %iota_compare_fusion.6), kind=kOutput, calls=%fused_computation.2 | convolution fusion | flops 412114944 | bytes 18876096 | tf_op jit(solution)/shard_map/ckn,ckbj->nbcj/dot_general | solution.py:27
  730.3 18.9 %copy.40 = bf16[64,128,6,128]{1,0,3,2:T(8,128)(2,1)} copy(bf16[64,128,6,128]{3,0,1,2:T(8,128)(2,1)} %convert_bitcast_fusion) | data formatting | bytes 25165824 | tf_op jit(solution)/shard_map/convert_element_type | solution.py:28
  749.2 19.1 %reshape_reshape.6 = bf16[2,4,1024,768]{2,1,0,3:T(4,128)(2,1)} reshape(bf16[64,128,6,128]{1,0,3,2:T(8,128)(2,1)} %copy.40) | data formatting | bytes 25165824 | tf_op jit(solution)/shard_map/reshape;reshape | solution.py:66
  768.3 40.8 %fusion.17 = (bf16[2,1,1024,768]{2,1,0,3:T(2,128)(2,1)}, bf16[2,1,1024,768]{2,1,0,3:T(2,128)(2,1)}, bf16[2,1,1024,768]{2,1,0,3:T(2,128)(2,1)}, bf16[2,1,1024,768]{2,1,0,3:T(2,128)(2,1)}) fusion(bf16[2,4,1024,768]{2,1,0,3:T(4,128)(2,1)} %reshape_reshape.6), kind=kLoop, calls=%fused_computation.41 | loop fusion | bytes 25165824 | tf_op jit(solution)/shard_map/slice | solution.py:71
  809.1 15.2 %copy.41 = bf16[2,1,1024,768]{3,2,0,1:T(8,128)(2,1)} copy(bf16[2,1,1024,768]{2,1,0,3:T(2,128)(2,1)} %get-tuple-element.9) | data formatting | bytes 6291456 | tf_op jit(solution)/shard_map/slice | solution.py:71
  824.3 16.1 %copy.42 = bf16[2,1,1024,768]{3,2,0,1:T(8,128)(2,1)} copy(bf16[2,1,1024,768]{2,1,0,3:T(2,128)(2,1)} %get-tuple-element.8) | data formatting | bytes 6291456 | tf_op jit(solution)/shard_map/slice | solution.py:71
  840.4 15.2 %copy.43 = bf16[2,1,1024,768]{3,2,0,1:T(8,128)(2,1)} copy(bf16[2,1,1024,768]{2,1,0,3:T(2,128)(2,1)} %get-tuple-element.7) | data formatting | bytes 6291456 | tf_op jit(solution)/shard_map/slice | solution.py:71
  855.6 13.3 %copy.44 = bf16[2,1,1024,768]{3,2,0,1:T(8,128)(2,1)S(1)} copy(bf16[2,1,1024,768]{2,1,0,3:T(2,128)(2,1)} %get-tuple-element.6) | data formatting | bytes 6291456 | tf_op jit(solution)/shard_map/slice | solution.py:71
  868.9 20.6 %fusion.19 = f32[768,4096]{1,0:T(8,128)} fusion(bf16[2048,768]{1,0:T(8,128)(2,1)} %bitcast.54, bf16[2048,4096]{1,0:T(8,128)(2,1)} %all-gather.14.cloned.1.call-done), kind=kOutput, calls=%fused_computation.43 | convolution fusion | flops 12884901888 | bytes 32505856 | tf_op jit(solution)/shard_map/dot_general | solution.py:72
  889.5 20.4 %fusion.20 = f32[768,4096]{1,0:T(8,128)} fusion(bf16[2048,768]{1,0:T(8,128)(2,1)} %bitcast.53, bf16[2048,4096]{1,0:T(8,128)(2,1)} %all-gather.18.cloned.1.call-done), kind=kOutput, calls=%fused_computation.44 | convolution fusion | flops 12884901888 | bytes 32505856 | tf_op jit(solution)/shard_map/dot_general | solution.py:72
  909.9 20.7 %fusion.21 = f32[768,4096]{1,0:T(8,128)} fusion(bf16[2048,768]{1,0:T(8,128)(2,1)} %bitcast.52, bf16[2048,4096]{1,0:T(8,128)(2,1)} %all-gather.22.cloned.1.call-done), kind=kOutput, calls=%fused_computation.45 | convolution fusion | flops 12884901888 | bytes 32505856 | tf_op jit(solution)/shard_map/dot_general | solution.py:72
  930.6 29.1 %add_bitcast_fusion = f32[4096,768]{0,1:T(8,128)} fusion(f32[768,4096]{1,0:T(8,128)} %fusion.21, f32[768,4096]{1,0:T(8,128)} %fusion.19, f32[768,4096]{1,0:T(8,128)} %fusion.20, bf16[2048,768]{1,0:T(8,128)(2,1)S(1)} %bitcast.50, bf16[2048,4096]{1,0:T(8,128)(2,1)} %all-gather.26.cloned.1.call-done), kind=kOutput, calls=%fused_computation.1 | convolution fusion | flops 12894339072 | bytes 70254592 | tf_op jit(solution)/shard_map/dot_general | solution.py:72
  959.7 95.8 %collective-permute-start.2 = (f32[4096,768]{0,1:T(8,128)}, f32[4096,768]{0,1:T(8,128)}, u32[]{:S(2)}, u32[]{:S(2)}) collective-permute-start(f32[4096,768]{0,1:T(8,128)} %add_bitcast_fusion), channel_id=1, source_target_pairs={{0,0},{16,1},{1,16},{17,17},{2,2},{18,3},{3,18},{19,19},{4,4},{20,... | collective-permute-start | bytes 37748744 | tf_op jit(solution)/shard_map/ppermute | solution.py:76
  1056.2 7.1 convert_bitcast_fusion.1
  1068.3 12.7 copy.45
  1081.1 14.1 %fusion.22 = f32[6,128,128]{2,1,0:T(8,128)} fusion(bf16[4096,6,128]{2,0,1:T(8,128)(2,1)} %bitcast.51, f32[4096,6,128]{0,2,1:T(8,128)} %bitcast.11), kind=kOutput, calls=%fused_computation.46 | convolution fusion | flops 4831838208 | bytes 19267584 | tf_op jit(solution)/shard_map/nca,ncb->cab/dot_general | solution.py:85
  1095.2 11.7 multiply_multiply_fusion
  1106.9 178.3 %all-reduce.2.cloned.1.call-done = f32[6,128,128]{2,1,0:T(8,128)} async-done(((f32[6,128,128]{2,1,0:T(8,128)}), f32[6,128,128]{2,1,0:T(8,128)}) %all-reduce.2.cloned.1.call-update) | async-done | bytes 393232 | tf_op jit(solution)/shard_map/psum | solution.py:89
  (56 shorter events, 16.3 us)
Async XLA Ops:
  7.2 173.0 %all-gather.12.cloned.1.call-start = ((), (), s32[]{:S(2)}) async-start(), calls=%async_computation.1 | async-start | bytes 9437184 | tf_op jit(solution)/shard_map/all_gather | solution.py:69
  11.5 340.2 %all-gather.16.cloned.1.call-start = ((), (), s32[]{:S(2)}) async-start(), calls=%async_computation.3 | async-start | bytes 9437184 | tf_op jit(solution)/shard_map/all_gather | solution.py:69
  12.3 511.1 %all-gather.20.cloned.1.call-start = ((), (), s32[]{:S(2)}) async-start(), calls=%async_computation.5 | async-start | bytes 9437184 | tf_op jit(solution)/shard_map/all_gather | solution.py:69
  13.0 532.7 %all-gather.10.cloned.1.call-start = ((), (), s32[]{:S(2)}) async-start(), calls=%async_computation | async-start | bytes 9437184 | tf_op jit(solution)/shard_map/all_gather | solution.py:53
  13.6 701.1 %all-gather.24.cloned.1.call-start = ((), (), s32[]{:S(2)}) async-start(), calls=%async_computation.7 | async-start | bytes 9437184 | tf_op jit(solution)/shard_map/all_gather | solution.py:69
  14.2 854.8 %all-gather.14.cloned.1.call-start = ((), (), s32[]{:S(2)}) async-start(), calls=%async_computation.2 | async-start | bytes 25165824 | tf_op jit(solution)/shard_map/all_gather | solution.py:70
  180.2 709.3 %all-gather.18.cloned.1.call-start = ((), (), s32[]{:S(2)}) async-start(), calls=%async_computation.4 | async-start | bytes 25165824 | tf_op jit(solution)/shard_map/all_gather | solution.py:70
  351.8 558.1 %all-gather.22.cloned.1.call-start = ((), (), s32[]{:S(2)}) async-start(), calls=%async_computation.6 | async-start | bytes 25165824 | tf_op jit(solution)/shard_map/all_gather | solution.py:70
  523.3 191.4 %copy-start.4 = (s32[6]{0:T(128)S(1)}, s32[6]{0:T(128)}, u32[]{:S(2)}) copy-start(s32[6]{0:T(128)} %param.11) | copy-start | bytes 76
  523.3 191.5 %copy-start.2 = (s32[6]{0:T(128)S(1)}, s32[6]{0:T(128)}, u32[]{:S(2)}) copy-start(s32[6]{0:T(128)} %param.12) | copy-start | bytes 76
  523.3 191.6 %copy-start.1 = (s32[6,32]{1,0:T(8,128)S(1)}, s32[6,32]{1,0:T(8,128)}, u32[]{:S(2)}) copy-start(s32[6,32]{1,0:T(8,128)} %param.10) | copy-start | bytes 2308
  523.3 192.6 %copy-start.3 = (s32[64]{0:T(128)S(1)}, s32[64]{0:T(128)}, u32[]{:S(2)}) copy-start(s32[64]{0:T(128)} %param.13) | copy-start | bytes 772
  523.4 407.2 %all-gather.26.cloned.1.call-start = ((), (), s32[]{:S(2)}) async-start(), calls=%async_computation.8 | async-start | bytes 25165824 | tf_op jit(solution)/shard_map/all_gather | solution.py:70
  545.7 170.8 %collective-permute-start.1 = (bf16[6,4096,128]{2,1,0:T(8,128)(2,1)}, bf16[6,4096,128]{2,1,0:T(8,128)(2,1)}, u32[]{:S(2)}, u32[]{:S(2)}) collective-permute-start(bf16[6,4096,128]{2,1,0:T(8,128)(2,1)} %all-gather.10.cloned.1.call-done), channel_id=1, source_target_pairs={{0,0},{16,1},{1,16},{17,17},{2,2},{18,3},{3,18},{19,19},{4,4},{20,... | collective-permute-start | bytes 18874376 | tf_op jit(solution)/shard_map/ppermute | solution.py:54
  714.7 570.5 %all-reduce.2.cloned.1.call-start = ((), (), s32[]{:S(2)}) async-start(), calls=%async_computation.9 | async-start | bytes 786432 | tf_op jit(solution)/shard_map/psum | solution.py:89
  715.0 0.7 collective-permute-start
  959.7 108.6 %collective-permute-start.2 = (f32[4096,768]{0,1:T(8,128)}, f32[4096,768]{0,1:T(8,128)}, u32[]{:S(2)}, u32[]{:S(2)}) collective-permute-start(f32[4096,768]{0,1:T(8,128)} %add_bitcast_fusion), channel_id=1, source_target_pairs={{0,0},{16,1},{1,16},{17,17},{2,2},{18,3},{3,18},{19,19},{4,4},{20,... | collective-permute-start | bytes 37748744 | tf_op jit(solution)/shard_map/ppermute | solution.py:76
  1095.2 190.1 %copy-start = (f32[6,64,128]{2,1,0:T(8,128)S(1)}, f32[6,64,128]{2,1,0:T(8,128)}, u32[]{:S(2)}) copy-start(f32[6,64,128]{2,1,0:T(8,128)} %param.9) | copy-start | bytes 589828
Sparse Core Ops, SparseCore 0:
  11.6 168.5 all-gather.11
  181.7 169.9 all-gather.15
  353.3 169.9 all-gather.19
  524.7 20.9 all-gather.9
  547.6 166.9 all-gather.23
  716.1 32.0 all-gather.13
  749.8 31.2 all-gather.17
  782.6 31.2 all-gather.21
  815.4 31.2 all-gather.25
  1095.3 189.8 all-reduce.1

commit v2 on v0

--- a/solution.py
+++ b/solution.py
@@ -7,6 +7,7 @@
 KMAX = 32
 WJ = 128
 NB = 64
+GATHER_CHUNKS = 4
 
 
 def slot_table(block_list, block_count, child_width, owner_slot):
@@ -44,11 +45,19 @@
     blocks = gathered.reshape(children, KMAX, B, WJ)
     blocks = jnp.where(active_columns[:, None, None, :], blocks, jnp.zeros_like(blocks))
     panel_rows = expand_rows(place_bf, blocks)
-    product = jnp.dot(
-        lax.all_gather(ancestor_sigma, "snode", axis=1, tiled=True),
-        panel_rows,
-        preferred_element_type=jnp.float32,
-    )
+    snode_devices = lax.axis_size("snode")
+    own_cols = ancestor_sigma.shape[1]
+    chunk = own_cols // GATHER_CHUNKS
+    flipped = ancestor_sigma.T
+    rows_by_chunk = panel_rows.reshape(snode_devices, GATHER_CHUNKS, chunk, children * WJ)
+    product = None
+    for q in range(GATHER_CHUNKS):
+        piece = lax.all_gather(flipped[q * chunk : (q + 1) * chunk], "snode", axis=0, tiled=True)
+        rows_q = rows_by_chunk[:, q].reshape(snode_devices * chunk, children * WJ)
+        part = lax.dot_general(
+            piece, rows_q, (((0,), (0,)), ((), ())), preferred_element_type=jnp.float32
+        )
+        product = part if product is None else product + part
     product_table = product.reshape(local_rows, children, WJ)
     own_blocks = local_rows // B
     own_table = lax.dynamic_slice_in_dim(place_bf, row_positions * own_blocks, own_blocks, 2)

time: 928 us -> 1120 us (1.21)
  waiting for transfers between devices: 714 us -> 892 us
  local copies, waits for them, and re-layouts: 36.7 us -> 68 us
  matrix products: 146 us -> 125 us
    all_gather x1 -> x4, waiting for transfers between devices: 690 us -> 872 us  [body(): lax.all_gather(flipped[q * chunk:(q + 1) * chunk], 'snode', axis=0, tiled...]
    slice x0 -> x6, local copies, waits for them, and re-layouts: none -> 30.3 us  [the longest x5 26 us: body(): rows_q = rows_by_chunk[:, q].reshape(snode_devices * chunk, children * WJ)]
    dot_general x1 -> x4, matrix products: 118 us -> 88.5 us  [body(): lax.dot_general(piece, rows_q, (((0,), (0,)), ((), ())), preferred_elemen...]
  transfers between devices with their start and end apart: 3 -> 6, of which waited for: 3 -> 6; matrix products, arithmetic and copies ran while one was open for 6% -> 14% of each run, Pallas kernels for 0% -> 0%
where the time goes in v2:
time: 1120 us; the launch traced here: 1110 us
  waiting for transfers between devices  892 us (80%)
  matrix products  125 us (11%)
  local copies, waits for them, and re-layouts  68 us (6%)
  between operations  14.5 us (1%)
  other arithmetic  14 us (1%)
    all_gather x4, waiting for transfers between devices, body(): lax.all_gather(flipped[q * chunk:(q + 1) * chunk], 'snode', axis=0, tiled...  872 us
    dot_general x4, matrix products, body(): lax.dot_general(piece, rows_q, (((0,), (0,)), ((), ())), preferred_elemen...  88.5 us
    slice x5, local copies, waits for them, and re-layouts, body(): rows_q = rows_by_chunk[:, q].reshape(snode_devices * chunk, children * WJ)  26 us
    convert_element_type x2, local copies, waits for them, and re-layouts, expand_rows(): spread.astype(jnp.bfloat16).reshape(place_table.shape[2] * B, children * WJ)  22.7 us
    dot_general x2, matrix products, expand_rows(): jnp.einsum('ckn,ckbj->nbcj', place_table, blocks, preferred_element_type=...  22.6 us
  transfers between devices with their start and end apart: 6, of which 6 were waited for; matrix products, arithmetic and copies ran while one was open for 14% of the time, Pallas kernels for 0%

profile of v2, /device:TPU:0, one launch (start us, length us, event | category | flops | bytes accessed | tf_op | source)
XLA Modules:
  0.0 1113.8 jit_solution(2139051503852774396)
XLA Ops:
  8.0 4.3 fusion.13
  17.1 12.0 %all-gather.6.cloned.1.call-done = bf16[6,4096,128]{2,1,0:T(8,128)(2,1)} async-done(((bf16[6,2048,128]{2,1,0:T(8,128)(2,1)}), bf16[6,4096,128]{2,1,0:T(8,128)(2,1)}) %all-gather.6.cloned.1.call-update) | async-done | bytes 6291472 | tf_op jit(solution)/shard_map/all_gather | solution.py:44
  29.0 15.5 %convert_bitcast_fusion = bf16[64,128,6,128]{3,0,1,2:T(8,128)(2,1)} fusion(bf16[6,32,128,128]{3,2,1,0:T(8,128)(2,1)} %bitcast.48, pred[6,128]{1,0:T(8,128)(4,1)S(1)} %get-tuple-element.11, s32[6,32]{1,0:T(8,128)S(1)} %select_reduce_fusion, pred[6,32]{1,0:T(8,128)(4,1)S(1)} %iota_compare_fusion.2), kind=kOutput, calls=%fused_computation.2 | convolution fusion | flops 412114944 | bytes 18876096 | tf_op jit(solution)/shard_map/ckn,ckbj->nbcj/dot_general | solution.py:25
  44.5 17.6 %copy.33 = bf16[64,128,6,128]{1,3,2,0:T(8,128)(2,1)} copy(bf16[64,128,6,128]{3,0,1,2:T(8,128)(2,1)} %convert_bitcast_fusion) | data formatting | bytes 25165824 | tf_op jit(solution)/shard_map/convert_element_type | solution.py:26
  62.1 8.9 fusion.12
  71.0 4.7 copy.34
  75.7 4.7 copy.35
  80.4 4.7 copy.36
  85.1 3.0 copy.37
  88.1 7.1 convert_bitcast_fusion.1
  95.2 5.1 copy.39
  100.4 182.2 %all-gather.8.cloned.1.call-done = bf16[2048,4096]{0,1:T(8,128)(2,1)} async-done(((bf16[128,4096]{0,1:T(8,128)(2,1)}), bf16[2048,4096]{0,1:T(8,128)(2,1)}) %all-gather.8.cloned.1.call-update) | async-done | bytes 16777232 | tf_op jit(solution)/shard_map/all_gather | solution.py:55
  282.6 20.7 %fusion.14 = f32[768,4096]{1,0:T(8,128)} fusion(bf16[2048,768]{1,0:T(8,128)(2,1)} %bitcast.54, bf16[2048,4096]{0,1:T(8,128)(2,1)} %all-gather.8.cloned.1.call-done), kind=kOutput, calls=%fused_computation.29 | convolution fusion | flops 12884901888 | bytes 32505856 | tf_op jit(solution)/shard_map/dot_general | solution.py:57
  303.3 229.9 %all-gather.10.cloned.1.call-done = bf16[2048,4096]{0,1:T(8,128)(2,1)} async-done(((bf16[128,4096]{0,1:T(8,128)(2,1)}), bf16[2048,4096]{0,1:T(8,128)(2,1)}) %all-gather.10.cloned.1.call-update) | async-done | bytes 16777232 | tf_op jit(solution)/shard_map/all_gather | solution.py:55
  533.1 19.9 %fusion.15 = f32[768,4096]{1,0:T(8,128)} fusion(bf16[2048,768]{1,0:T(8,128)(2,1)S(1)} %bitcast.53, bf16[2048,4096]{0,1:T(8,128)(2,1)} %all-gather.10.cloned.1.call-done), kind=kOutput, calls=%fused_computation.30 | convolution fusion | flops 12884901888 | bytes 32505856 | tf_op jit(solution)/shard_map/dot_general | solution.py:57
  553.0 230.5 %all-gather.12.cloned.1.call-done = bf16[2048,4096]{0,1:T(8,128)(2,1)} async-done(((bf16[128,4096]{0,1:T(8,128)(2,1)}), bf16[2048,4096]{0,1:T(8,128)(2,1)}) %all-gather.12.cloned.1.call-update) | async-done | bytes 16777232 | tf_op jit(solution)/shard_map/all_gather | solution.py:55
  783.6 20.7 %fusion.16 = f32[768,4096]{1,0:T(8,128)} fusion(bf16[2048,768]{1,0:T(8,128)(2,1)} %bitcast.52, bf16[2048,4096]{0,1:T(8,128)(2,1)} %all-gather.12.cloned.1.call-done), kind=kOutput, calls=%fused_computation.31 | convolution fusion | flops 12884901888 | bytes 32505856 | tf_op jit(solution)/shard_map/dot_general | solution.py:57
  804.3 229.7 %all-gather.14.cloned.1.call-done = bf16[2048,4096]{0,1:T(8,128)(2,1)} async-done(((bf16[128,4096]{0,1:T(8,128)(2,1)}), bf16[2048,4096]{0,1:T(8,128)(2,1)}) %all-gather.14.cloned.1.call-update) | async-done | bytes 16777232 | tf_op jit(solution)/shard_map/all_gather | solution.py:55
  1034.0 27.2 %add_add_fusion = f32[768,4096]{1,0:T(8,128)} fusion(f32[768,4096]{1,0:T(8,128)} %fusion.16, f32[768,4096]{1,0:T(8,128)} %fusion.14, f32[768,4096]{1,0:T(8,128)} %fusion.15, bf16[2048,768]{1,0:T(8,128)(2,1)S(1)} %bitcast.51, bf16[2048,4096]{0,1:T(8,128)(2,1)} %all-gather.14.cloned.1.call-done), kind=kOutput, calls=%fused_computation.1 | convolution fusion | flops 12894339072 | bytes 70254592 | tf_op jit(solution)/shard_map/dot_general | solution.py:57
  1061.2 12.8 %copy.38 = f32[4096,6,128]{2,0,1:T(8,128)} copy(f32[4096,6,128]{0,2,1:T(8,128)} %bitcast.44) | data formatting | bytes 25165824 | tf_op jit(solution)/shard_map/reshape | solution.py:61
  1074.0 14.1 %fusion.17 = f32[6,128,128]{2,1,0:T(8,128)} fusion(bf16[4096,6,128]{2,0,1:T(8,128)(2,1)} %bitcast.47, f32[4096,6,128]{0,2,1:T(8,128)} %bitcast.45), kind=kOutput, calls=%fused_computation.32 | convolution fusion | flops 4831838208 | bytes 19267584 | tf_op jit(solution)/shard_map/nca,ncb->cab/dot_general | solution.py:65
  1088.2 11.7 %multiply_multiply_fusion = f32[4096,6,128]{2,0,1:T(8,128)} fusion(f32[4096,6,128]{2,0,1:T(8,128)} %copy.38, f32[6,128]{1,0:T(8,128)S(1)} %copy-done.5, f32[4096,6]{0,1:T(8,128)S(1)} %bitcast.55), kind=kLoop, calls=%fused_computation | loop fusion | flops 9437184 | bytes 25267200 | tf_op jit(solution)/shard_map/mul | solution.py:85
  1099.9 5.1 all-reduce.2.cloned.1.call-done
  1105.0 1.7 multiply_multiply_fusion.1
  (43 shorter events, 5.4 us)
Async XLA Ops:
  7.2 21.9 %all-gather.6.cloned.1.call-start = ((), (), s32[]{:S(2)}) async-start(), calls=%async_computation | async-start | bytes 9437184 | tf_op jit(solution)/shard_map/all_gather | solution.py:44
  7.9 274.7 %all-gather.8.cloned.1.call-start = ((), (), s32[]{:S(2)}) async-start(), calls=%async_computation.1 | async-start | bytes 17825792 | tf_op jit(solution)/shard_map/all_gather | solution.py:55
  7.9 6.4 copy-start.7
  8.0 6.4 copy-start.8
  8.0 6.6 copy-start.10
  8.0 7.7 copy-start.9
  12.3 520.8 %all-gather.10.cloned.1.call-start = ((), (), s32[]{:S(2)}) async-start(), calls=%async_computation.2 | async-start | bytes 17825792 | tf_op jit(solution)/shard_map/all_gather | solution.py:55
  13.1 770.5 %all-gather.12.cloned.1.call-start = ((), (), s32[]{:S(2)}) async-start(), calls=%async_computation.3 | async-start | bytes 17825792 | tf_op jit(solution)/shard_map/all_gather | solution.py:55
  13.7 1020.3 %all-gather.14.cloned.1.call-start = ((), (), s32[]{:S(2)}) async-start(), calls=%async_computation.4 | async-start | bytes 17825792 | tf_op jit(solution)/shard_map/all_gather | solution.py:55
  14.2 1090.8 %all-reduce.2.cloned.1.call-start = ((), (), s32[]{:S(2)}) async-start(), calls=%async_computation.5 | async-start | bytes 786432 | tf_op jit(solution)/shard_map/psum | solution.py:69
  15.8 0.6 copy-start.4
  282.6 250.6 %copy-start.1 = (bf16[16,1,128,768]{3,2,0,1:T(8,128)(2,1)S(1)}, bf16[16,1,128,768]{3,2,0,1:T(8,128)(2,1)}, u32[]{:S(2)}) copy-start(bf16[16,1,128,768]{3,2,0,1:T(8,128)(2,1)} %copy.35) | copy-start | bytes 9437188
  783.6 250.4 %copy-start = (bf16[16,1,128,768]{3,2,0,1:T(8,128)(2,1)S(1)}, bf16[16,1,128,768]{3,2,0,1:T(8,128)(2,1)}, u32[]{:S(2)}) copy-start(bf16[16,1,128,768]{3,2,0,1:T(8,128)(2,1)} %copy.37) | copy-start | bytes 9437188
  1074.0 14.2 %copy-start.2 = (f32[1,6,32,128]{3,1,2,0:T(8,128)S(1)}, f32[1,6,32,128]{3,1,2,0:T(8,128)}, u32[]{:S(2)}) copy-start(f32[1,6,32,128]{3,1,2,0:T(8,128)} %copy.55) | copy-start | bytes 294916
  1074.0 14.2 %copy-start.5 = (f32[6,128]{1,0:T(8,128)S(1)}, f32[6,128]{1,0:T(8,128)}, u32[]{:S(2)}) copy-start(f32[6,128]{1,0:T(8,128)} %copy-done.4) | copy-start | bytes 9220
  1088.2 16.8 %copy-start.3 = (f32[6,64,128]{2,1,0:T(8,128)S(1)}, f32[6,64,128]{2,1,0:T(8,128)}, u32[]{:S(2)}) copy-start(f32[6,64,128]{2,1,0:T(8,128)} %param.9) | copy-start | bytes 589828
  1088.2 16.8 %copy-start.6 = (f32[6,64]{1,0:T(8,128)S(1)}, f32[6,64]{1,0:T(8,128)}, u32[]{:S(2)}) copy-start(f32[6,64]{1,0:T(8,128)} %constant_dynamic-slice_fusion) | copy-start | bytes 4612
Sparse Core Ops, SparseCore 0:
  9.5 19.4 all-gather.5
  31.7 250.7 all-gather.7
  285.3 247.8 all-gather.9
  535.7 247.8 all-gather.11
  786.1 247.8 all-gather.13
  1088.3 16.6 all-reduce.1

commit v3 on v0

--- a/solution.py
+++ b/solution.py
@@ -44,9 +44,36 @@
     blocks = gathered.reshape(children, KMAX, B, WJ)
     blocks = jnp.where(active_columns[:, None, None, :], blocks, jnp.zeros_like(blocks))
     panel_rows = expand_rows(place_bf, blocks)
+    snode_devices = lax.axis_size("snode")
+    snode_position = lax.axis_index("snode")
+    own_cols = ancestor_sigma.shape[1]
+    half = own_cols // 2
+    by_block = panel_rows.reshape(snode_devices, own_cols, children * WJ)
+    gathered_half = lax.all_gather(ancestor_sigma[:, :half], "snode", axis=1, tiled=True)
     product = jnp.dot(
-        lax.all_gather(ancestor_sigma, "snode", axis=1, tiled=True),
-        panel_rows,
+        gathered_half,
+        by_block[:, :half].reshape(snode_devices * half, children * WJ),
+        preferred_element_type=jnp.float32,
+    )
+    rest = ancestor_sigma[:, half:]
+    pieces = []
+    rows = []
+    for shift in range(snode_devices):
+        if shift == 0:
+            pieces.append(rest)
+        else:
+            pieces.append(
+                lax.ppermute(
+                    rest, "snode", [(i, (i + shift) % snode_devices) for i in range(snode_devices)]
+                )
+            )
+        source = (snode_position - shift) % snode_devices
+        rows.append(
+            lax.dynamic_slice_in_dim(panel_rows, source * own_cols + half, own_cols - half, 0)
+        )
+    product = product + jnp.dot(
+        jnp.concatenate(pieces, axis=1),
+        jnp.concatenate(rows, axis=0),
         preferred_element_type=jnp.float32,
     )
     product_table = product.reshape(local_rows, children, WJ)

time: 928 us -> 1540 us (1.66)
  starting transfers between devices: 0.11 us -> 485 us
  local copies, waits for them, and re-layouts: 36.7 us -> 133 us
  waiting for transfers between devices: 714 us -> 785 us
  matrix products: 146 us -> 108 us
    all_gather x1, waiting for transfers between devices: 690 us -> 0.01 us  [body(): lax.all_gather(ancestor_sigma[:, :half], 'snode', axis=1, tiled=True)]
    ppermute x0 -> x15, waiting for transfers between devices: none -> 652 us  [body(): lax.ppermute(rest, 'snode', [(i, (i + shift) % snode_devices) for i in ra...]
    ppermute x0 -> x15, starting transfers between devices: none -> 485 us  [body(): lax.ppermute(rest, 'snode', [(i, (i + shift) % snode_devices) for i in ra...]
    psum x1, waiting for transfers between devices: 5.09 us -> 132 us  [body(): reduced_total = lax.psum(partial_value, 'row')]
    unnamed x8 -> x51, local copies, waits for them, and re-layouts: 0.16 us -> 63.7 us
    dot_general x1 -> x2, matrix products: 118 us -> 68.1 us  [the longest x1 34.5 us: body(): jnp.dot(jnp.concatenate(pieces, axis=1), jnp.concatenate(rows, axis=0), p...]
    another operation x0 -> x1, local copies, waits for them, and re-layouts: none -> 20.2 us  [body(): by_block = panel_rows.reshape(snode_devices, own_cols, children * WJ)]
    all_gather x1, waiting for transfers between devices: 17.4 us -> 0.01 us  [body(): gathered = lax.all_gather(child_panels, 'row', axis=1, tiled=True)]
  transfers between devices with their start and end apart: 3 -> 18, of which waited for: 3 -> 6; matrix products, arithmetic and copies ran while one was open for 6% -> 10% of each run, Pallas kernels for 0% -> 0%
where the time goes in v3:
time: 1540 us
  waiting for transfers between devices  785 us (51%)
  starting transfers between devices  485 us (31%)
  local copies, waits for them, and re-layouts  133 us (9%)
  matrix products  108 us (7%)
    ppermute x15, waiting for transfers between devices, body(): lax.ppermute(rest, 'snode', [(i, (i + shift) % snode_devices) for i in ra...  652 us
    ppermute x15, starting transfers between devices, body(): lax.ppermute(rest, 'snode', [(i, (i + shift) % snode_devices) for i in ra...  485 us
    psum x1, waiting for transfers between devices, body(): reduced_total = lax.psum(partial_value, 'row')  132 us
    unnamed x51, local copies, waits for them, and re-layouts  63.7 us
    dot_general x1, matrix products, body(): jnp.dot(jnp.concatenate(pieces, axis=1), jnp.concatenate(rows, axis=0), p...  34.5 us
    dot_general x1, matrix products, body(): jnp.dot(gathered_half, by_block[:, :half].reshape(snode_devices * half, c...  33.6 us
  transfers between devices with their start and end apart: 18, of which 6 were waited for; matrix products, arithmetic and copies ran while one was open for 10% of the time, Pallas kernels for 0%

profile of v3, /device:TPU:0, one launch (start us, length us, event | category | flops | bytes accessed | tf_op | source)
XLA Modules:
  0.0 1539.3 jit_solution(18334661826244284324)
XLA Ops:
  25.4 127.9 %collective-permute-done = bf16[4096,256]{1,0:T(8,128)(2,1)} collective-permute-done((bf16[4096,256]{1,0:T(8,128)(2,1)S(1)}, bf16[4096,256]{1,0:T(8,128)(2,1)}, u32[]{:S(2)}, u32[]{:S(2)}) %collective-permute-start) | collective-permute-done | bytes 2097184 | tf_op jit(solution)/shard_map/ppermute | solution.py:66
  153.3 45.3 %collective-permute-start.5 = (bf16[4096,256]{1,0:T(8,128)(2,1)S(1)}, bf16[4096,256]{1,0:T(8,128)(2,1)S(1)}, u32[]{:S(2)}, u32[]{:S(2)}) collective-permute-start(bf16[4096,256]{1,0:T(8,128)(2,1)S(1)} %get-tuple-element.2), channel_id=1, source_target_pairs={{0,12},{2,14},{4,16},{6,18},{8,20},{10,22},{12,24},{14,26},{16,28}... | collective-permute-start | bytes 6291464 | tf_op jit(solution)/shard_map/ppermute | solution.py:66
  201.7 22.5 %collective-permute-start.6 = (bf16[4096,256]{1,0:T(8,128)(2,1)S(1)}, bf16[4096,256]{1,0:T(8,128)(2,1)S(1)}, u32[]{:S(2)}, u32[]{:S(2)}) collective-permute-start(bf16[4096,256]{1,0:T(8,128)(2,1)S(1)} %get-tuple-element.2), channel_id=1, source_target_pairs={{0,14},{2,16},{4,18},{6,20},{8,22},{10,24},{12,26},{14,28},{16,30}... | collective-permute-start | bytes 6291464 | tf_op jit(solution)/shard_map/ppermute | solution.py:66
  227.3 164.2 %collective-permute-done.2 = bf16[4096,256]{1,0:T(8,128)(2,1)} collective-permute-done((bf16[4096,256]{1,0:T(8,128)(2,1)S(1)}, bf16[4096,256]{1,0:T(8,128)(2,1)}, u32[]{:S(2)}, u32[]{:S(2)}) %collective-permute-start.2) | collective-permute-done | bytes 2097184 | tf_op jit(solution)/shard_map/ppermute | solution.py:66
  397.7 238.2 %collective-permute-done.4 = bf16[4096,256]{1,0:T(8,128)(2,1)} collective-permute-done((bf16[4096,256]{1,0:T(8,128)(2,1)S(1)}, bf16[4096,256]{1,0:T(8,128)(2,1)}, u32[]{:S(2)}, u32[]{:S(2)}) %collective-permute-start.4) | collective-permute-done | bytes 2097184 | tf_op jit(solution)/shard_map/ppermute | solution.py:66
  639.0 72.9 %collective-permute-start.10 = (bf16[4096,256]{1,0:T(8,128)(2,1)S(1)}, bf16[4096,256]{1,0:T(8,128)(2,1)S(1)}, u32[]{:S(2)}, u32[]{:S(2)}) collective-permute-start(bf16[4096,256]{1,0:T(8,128)(2,1)S(1)} %get-tuple-element.2), channel_id=1, source_target_pairs={{0,22},{2,24},{4,26},{6,28},{8,30},{10,0},{12,2},{14,4},{16,6},{18... | collective-permute-start | bytes 6291464 | tf_op jit(solution)/shard_map/ppermute | solution.py:66
  713.4 182.4 %collective-permute-start.11 = (bf16[4096,256]{1,0:T(8,128)(2,1)S(1)}, bf16[4096,256]{1,0:T(8,128)(2,1)S(1)}, u32[]{:S(2)}, u32[]{:S(2)}) collective-permute-start(bf16[4096,256]{1,0:T(8,128)(2,1)S(1)} %get-tuple-element.2), channel_id=1, source_target_pairs={{0,24},{2,26},{4,28},{6,30},{8,0},{10,2},{12,4},{14,6},{16,8},{18,... | collective-permute-start | bytes 6291464 | tf_op jit(solution)/shard_map/ppermute | solution.py:66
  899.3 87.8 %collective-permute-start.13 = (bf16[4096,256]{1,0:T(8,128)(2,1)S(1)}, bf16[4096,256]{1,0:T(8,128)(2,1)S(1)}, u32[]{:S(2)}, u32[]{:S(2)}) collective-permute-start(bf16[4096,256]{1,0:T(8,128)(2,1)S(1)} %get-tuple-element.2), channel_id=1, source_target_pairs={{0,28},{2,30},{4,0},{6,2},{8,4},{10,6},{12,8},{14,10},{16,12},{18,... | collective-permute-start | bytes 6291464 | tf_op jit(solution)/shard_map/ppermute | solution.py:66
  988.5 63.8 %collective-permute-start.14 = (bf16[4096,256]{1,0:T(8,128)(2,1)S(1)}, bf16[4096,256]{1,0:T(8,128)(2,1)S(1)}, u32[]{:S(2)}, u32[]{:S(2)}) collective-permute-start(bf16[4096,256]{1,0:T(8,128)(2,1)S(1)} %get-tuple-element.2), channel_id=1, source_target_pairs={{0,30},{2,0},{4,2},{6,4},{8,6},{10,8},{12,10},{14,12},{16,14},{18,... | collective-permute-start | bytes 6291464 | tf_op jit(solution)/shard_map/ppermute | solution.py:66
  1058.3 46.5 %collective-permute-done.13 = bf16[4096,256]{1,0:T(8,128)(2,1)S(1)} collective-permute-done((bf16[4096,256]{1,0:T(8,128)(2,1)S(1)}, bf16[4096,256]{1,0:T(8,128)(2,1)S(1)}, u32[]{:S(2)}, u32[]{:S(2)}) %collective-permute-start.13) | collective-permute-done | bytes 2097184 | tf_op jit(solution)/shard_map/ppermute | solution.py:66
  1106.2 75.1 %collective-permute-done.14 = bf16[4096,256]{1,0:T(8,128)(2,1)S(1)} collective-permute-done((bf16[4096,256]{1,0:T(8,128)(2,1)S(1)}, bf16[4096,256]{1,0:T(8,128)(2,1)S(1)}, u32[]{:S(2)}, u32[]{:S(2)}) %collective-permute-start.14) | collective-permute-done | bytes 2097184 | tf_op jit(solution)/shard_map/ppermute | solution.py:66
  1182.8 15.5 %convert_bitcast_fusion = bf16[64,128,6,128]{3,0,1,2:T(8,128)(2,1)} fusion(bf16[6,32,128,128]{3,2,1,0:T(8,128)(2,1)} %bitcast.70, pred[6,128]{1,0:T(8,128)(4,1)S(1)} %get-tuple-element.6, s32[6,32]{1,0:T(8,128)S(1)} %select_reduce_fusion, pred[6,32]{1,0:T(8,128)(4,1)S(1)} %iota_compare_fusion.2), kind=kOutput, calls=%fused_computation.3 | convolution fusion | flops 412114944 | bytes 18876096 | tf_op jit(solution)/shard_map/ckn,ckbj->nbcj/dot_general | solution.py:24
  1198.3 17.9 %copy.23 = bf16[64,128,6,128]{1,0,3,2:T(8,128)(2,1)} copy(bf16[64,128,6,128]{3,0,1,2:T(8,128)(2,1)} %convert_bitcast_fusion) | data formatting | bytes 25165824 | tf_op jit(solution)/shard_map/convert_element_type | solution.py:25
  1216.2 20.2 %reshape_reshape.6 = bf16[16,512,768]{1,0,2:T(8,128)(2,1)} reshape(bf16[64,128,6,128]{1,0,3,2:T(8,128)(2,1)} %copy.23) | data formatting | bytes 25165824 | tf_op jit(solution)/shard_map/reshape;reshape | solution.py:51
  1236.4 14.1 copy.45
  1253.3 6.8 copy.35
  1260.1 9.8 convert_bitcast_fusion.1
  1269.9 7.9 copy.26
  1291.7 33.6 %fusion.14 = f32[768,4096]{1,0:T(8,128)} fusion(bf16[4096,768]{0,1:T(8,128)(2,1)} %bitcast.72, bf16[4096,4096]{1,0:T(8,128)(2,1)} %all-gather.5.cloned.1.call-done), kind=kOutput, calls=%fused_computation.62 | convolution fusion | flops 25769803776 | bytes 52428800 | tf_op jit(solution)/shard_map/dot_general | solution.py:53
  1325.3 34.5 %bitcast_add_fusion = f32[4096,768]{0,1:T(8,128)} fusion(f32[768,4096]{1,0:T(8,128)} %fusion.14, bf16[4096,4096]{1,0:T(8,128)(2,1)} %constant_dynamic-update-slice_fusion, bf16[4096,768]{0,1:T(8,128)(2,1)} %dynamic-slice_dynamic-update-slice_fusion), kind=kOutput, calls=%fused_computation.1 | convolution fusion | flops 25772949504 | bytes 65011712 | tf_op jit(solution)/shard_map/dot_general | solution.py:74
  1359.8 12.8 copy.25
  1372.7 14.1 fusion.15
  1386.9 11.7 multiply_multiply_fusion
  1398.6 132.3 %all-reduce.2.cloned.1.call-done = f32[6,128,128]{2,1,0:T(8,128)} async-done(((f32[6,128,128]{2,1,0:T(8,128)}), f32[6,128,128]{2,1,0:T(8,128)}) %all-reduce.2.cloned.1.call-update) | async-done | bytes 393232 | tf_op jit(solution)/shard_map/psum | solution.py:87
  (89 shorter events, 67.0 us)
Async XLA Ops:
  7.2 1175.6 %all-gather.3.cloned.1.call-start = ((), (), s32[]{:S(2)}) async-start(), calls=%async_computation | async-start | bytes 9437184 | tf_op jit(solution)/shard_map/all_gather | solution.py:43
  7.9 15.0 copy-start.5
  7.9 15.0 copy-start.6
  7.9 16.7 %copy-start.7 = (s32[6]{0:T(128)S(1)}, s32[6]{0:T(128)}, u32[]{:S(2)}) copy-start(s32[6]{0:T(128)} %param.12) | copy-start | bytes 76
  7.9 1283.8 %all-gather.5.cloned.1.call-start = ((), (), s32[]{:S(2)}) async-start(), calls=%async_computation.1 | async-start | bytes 35651584 | tf_op jit(solution)/shard_map/all_gather | solution.py:52
  12.7 1518.1 %all-reduce.2.cloned.1.call-start = ((), (), s32[]{:S(2)}) async-start(), calls=%async_computation.2 | async-start | bytes 786432 | tf_op jit(solution)/shard_map/psum | solution.py:87
  12.7 140.6 %collective-permute-start = (bf16[4096,256]{1,0:T(8,128)(2,1)S(1)}, bf16[4096,256]{1,0:T(8,128)(2,1)}, u32[]{:S(2)}, u32[]{:S(2)}) collective-permute-start(bf16[4096,256]{1,0:T(8,128)(2,1)S(1)} %get-tuple-element.2), channel_id=1, source_target_pairs={{0,2},{2,4},{4,6},{6,8},{8,10},{10,12},{12,14},{14,16},{16,18},{18... | collective-permute-start | bytes 6291464 | tf_op jit(solution)/shard_map/ppermute | solution.py:66
  15.7 186.0 %collective-permute-start.1 = (bf16[4096,256]{1,0:T(8,128)(2,1)S(1)}, bf16[4096,256]{1,0:T(8,128)(2,1)}, u32[]{:S(2)}, u32[]{:S(2)}) collective-permute-start(bf16[4096,256]{1,0:T(8,128)(2,1)S(1)} %get-tuple-element.2), channel_id=1, source_target_pairs={{0,4},{2,6},{4,8},{6,10},{8,12},{10,14},{12,16},{14,18},{16,20},{1... | collective-permute-start | bytes 6291464 | tf_op jit(solution)/shard_map/ppermute | solution.py:66
  17.2 374.3 %collective-permute-start.2 = (bf16[4096,256]{1,0:T(8,128)(2,1)S(1)}, bf16[4096,256]{1,0:T(8,128)(2,1)}, u32[]{:S(2)}, u32[]{:S(2)}) collective-permute-start(bf16[4096,256]{1,0:T(8,128)(2,1)S(1)} %get-tuple-element.2), channel_id=1, source_target_pairs={{0,6},{2,8},{4,10},{6,12},{8,14},{10,16},{12,18},{14,20},{16,22},{... | collective-permute-start | bytes 6291464 | tf_op jit(solution)/shard_map/ppermute | solution.py:66
  19.7 374.9 %collective-permute-start.3 = (bf16[4096,256]{1,0:T(8,128)(2,1)S(1)}, bf16[4096,256]{1,0:T(8,128)(2,1)}, u32[]{:S(2)}, u32[]{:S(2)}) collective-permute-start(bf16[4096,256]{1,0:T(8,128)(2,1)S(1)} %get-tuple-element.2), channel_id=1, source_target_pairs={{0,8},{2,10},{4,12},{6,14},{8,16},{10,18},{12,20},{14,22},{16,24},... | collective-permute-start | bytes 6291464 | tf_op jit(solution)/shard_map/ppermute | solution.py:66
  21.2 614.6 %collective-permute-start.4 = (bf16[4096,256]{1,0:T(8,128)(2,1)S(1)}, bf16[4096,256]{1,0:T(8,128)(2,1)}, u32[]{:S(2)}, u32[]{:S(2)}) collective-permute-start(bf16[4096,256]{1,0:T(8,128)(2,1)S(1)} %get-tuple-element.2), channel_id=1, source_target_pairs={{0,10},{2,12},{4,14},{6,16},{8,18},{10,20},{12,22},{14,24},{16,26}... | collective-permute-start | bytes 6291464 | tf_op jit(solution)/shard_map/ppermute | solution.py:66
  24.7 369.9 %copy-start.2 = (f32[6,128]{1,0:T(8,128)}, f32[6,128]{1,0:T(8,128)S(1)}, u32[]{:S(2)}) copy-start(f32[6,128]{1,0:T(8,128)S(1)} %get-tuple-element.5) | copy-start | bytes 9220
  153.3 485.7 %collective-permute-start.5 = (bf16[4096,256]{1,0:T(8,128)(2,1)S(1)}, bf16[4096,256]{1,0:T(8,128)(2,1)S(1)}, u32[]{:S(2)}, u32[]{:S(2)}) collective-permute-start(bf16[4096,256]{1,0:T(8,128)(2,1)S(1)} %get-tuple-element.2), channel_id=1, source_target_pairs={{0,12},{2,14},{4,16},{6,18},{8,20},{10,22},{12,24},{14,26},{16,28}... | collective-permute-start | bytes 6291464 | tf_op jit(solution)/shard_map/ppermute | solution.py:66
  201.7 511.7 %collective-permute-start.6 = (bf16[4096,256]{1,0:T(8,128)(2,1)S(1)}, bf16[4096,256]{1,0:T(8,128)(2,1)S(1)}, u32[]{:S(2)}, u32[]{:S(2)}) collective-permute-start(bf16[4096,256]{1,0:T(8,128)(2,1)S(1)} %get-tuple-element.2), channel_id=1, source_target_pairs={{0,14},{2,16},{4,18},{6,20},{8,22},{10,24},{12,26},{14,28},{16,30}... | collective-permute-start | bytes 6291464 | tf_op jit(solution)/shard_map/ppermute | solution.py:66
  391.5 505.8 %collective-permute-start.7 = (bf16[4096,256]{1,0:T(8,128)(2,1)S(1)}, bf16[4096,256]{1,0:T(8,128)(2,1)S(1)}, u32[]{:S(2)}, u32[]{:S(2)}) collective-permute-start(bf16[4096,256]{1,0:T(8,128)(2,1)S(1)} %get-tuple-element.2), channel_id=1, source_target_pairs={{0,16},{2,18},{4,20},{6,22},{8,24},{10,26},{12,28},{14,30},{16,0},... | collective-permute-start | bytes 6291464 | tf_op jit(solution)/shard_map/ppermute | solution.py:66
  394.6 504.7 %collective-permute-start.8 = (bf16[4096,256]{1,0:T(8,128)(2,1)S(1)}, bf16[4096,256]{1,0:T(8,128)(2,1)S(1)}, u32[]{:S(2)}, u32[]{:S(2)}) collective-permute-start(bf16[4096,256]{1,0:T(8,128)(2,1)S(1)} %get-tuple-element.2), channel_id=1, source_target_pairs={{0,18},{2,20},{4,22},{6,24},{8,26},{10,28},{12,30},{14,0},{16,2},{... | collective-permute-start | bytes 6291464 | tf_op jit(solution)/shard_map/ppermute | solution.py:66
  635.9 352.7 %collective-permute-start.9 = (bf16[4096,256]{1,0:T(8,128)(2,1)S(1)}, bf16[4096,256]{1,0:T(8,128)(2,1)S(1)}, u32[]{:S(2)}, u32[]{:S(2)}) collective-permute-start(bf16[4096,256]{1,0:T(8,128)(2,1)S(1)} %get-tuple-element.2), channel_id=1, source_target_pairs={{0,20},{2,22},{4,24},{6,26},{8,28},{10,30},{12,0},{14,2},{16,4},{1... | collective-permute-start | bytes 6291464 | tf_op jit(solution)/shard_map/ppermute | solution.py:66
  639.0 414.8 %collective-permute-start.10 = (bf16[4096,256]{1,0:T(8,128)(2,1)S(1)}, bf16[4096,256]{1,0:T(8,128)(2,1)S(1)}, u32[]{:S(2)}, u32[]{:S(2)}) collective-permute-start(bf16[4096,256]{1,0:T(8,128)(2,1)S(1)} %get-tuple-element.2), channel_id=1, source_target_pairs={{0,22},{2,24},{4,26},{6,28},{8,30},{10,0},{12,2},{14,4},{16,6},{18... | collective-permute-start | bytes 6291464 | tf_op jit(solution)/shard_map/ppermute | solution.py:66
  713.4 341.9 %collective-permute-start.11 = (bf16[4096,256]{1,0:T(8,128)(2,1)S(1)}, bf16[4096,256]{1,0:T(8,128)(2,1)S(1)}, u32[]{:S(2)}, u32[]{:S(2)}) collective-permute-start(bf16[4096,256]{1,0:T(8,128)(2,1)S(1)} %get-tuple-element.2), channel_id=1, source_target_pairs={{0,24},{2,26},{4,28},{6,30},{8,0},{10,2},{12,4},{14,6},{16,8},{18,... | collective-permute-start | bytes 6291464 | tf_op jit(solution)/shard_map/ppermute | solution.py:66
  897.4 159.4 %collective-permute-start.12 = (bf16[4096,256]{1,0:T(8,128)(2,1)S(1)}, bf16[4096,256]{1,0:T(8,128)(2,1)S(1)}, u32[]{:S(2)}, u32[]{:S(2)}) collective-permute-start(bf16[4096,256]{1,0:T(8,128)(2,1)S(1)} %get-tuple-element.2), channel_id=1, source_target_pairs={{0,26},{2,28},{4,30},{6,0},{8,2},{10,4},{12,6},{14,8},{16,10},{18,... | collective-permute-start | bytes 6291464 | tf_op jit(solution)/shard_map/ppermute | solution.py:66
  899.3 205.4 %collective-permute-start.13 = (bf16[4096,256]{1,0:T(8,128)(2,1)S(1)}, bf16[4096,256]{1,0:T(8,128)(2,1)S(1)}, u32[]{:S(2)}, u32[]{:S(2)}) collective-permute-start(bf16[4096,256]{1,0:T(8,128)(2,1)S(1)} %get-tuple-element.2), channel_id=1, source_target_pairs={{0,28},{2,30},{4,0},{6,2},{8,4},{10,6},{12,8},{14,10},{16,12},{18,... | collective-permute-start | bytes 6291464 | tf_op jit(solution)/shard_map/ppermute | solution.py:66
  988.5 192.8 %collective-permute-start.14 = (bf16[4096,256]{1,0:T(8,128)(2,1)S(1)}, bf16[4096,256]{1,0:T(8,128)(2,1)S(1)}, u32[]{:S(2)}, u32[]{:S(2)}) collective-permute-start(bf16[4096,256]{1,0:T(8,128)(2,1)S(1)} %get-tuple-element.2), channel_id=1, source_target_pairs={{0,30},{2,0},{4,2},{6,4},{8,6},{10,8},{12,10},{14,12},{16,14},{18,... | collective-permute-start | bytes 6291464 | tf_op jit(solution)/shard_map/ppermute | solution.py:66
  1386.8 144.0 %copy-start.1 = (f32[6,64,128]{2,1,0:T(8,128)S(1)}, f32[6,64,128]{2,1,0:T(8,128)}, u32[]{:S(2)}) copy-start(f32[6,64,128]{2,1,0:T(8,128)} %param.9) | copy-start | bytes 589828
  1386.8 144.0 %copy-start.4 = (f32[6,64]{1,0:T(8,128)S(1)}, f32[6,64]{1,0:T(8,128)}, u32[]{:S(2)}) copy-start(f32[6,64]{1,0:T(8,128)} %constant_dynamic-slice_fusion.1) | copy-start | bytes 4612
  (4 other events, 46.1 us)
Sparse Core Ops, SparseCore 0:
  9.5 19.4 all-gather.2
  30.5 1254.7 all-gather.4
  1386.9 143.8 all-reduce.1

commit v4 on v0

--- a/solution.py
+++ b/solution.py
@@ -40,7 +40,14 @@
     local_rows = ancestor_sigma.shape[0]
     placed, active_columns = slot_table(block_list, block_count, child_width, owner_slot)
     place_bf = placed.astype(jnp.bfloat16)
-    gathered = lax.all_gather(child_panels, "row", axis=1, tiled=True)
+    if row_devices == 2:
+        partner = lax.ppermute(child_panels, "row", [(0, 1), (1, 0)])
+        first = row_positions == 0
+        gathered = jnp.concatenate(
+            [jnp.where(first, child_panels, partner), jnp.where(first, partner, child_panels)], axis=1
+        )
+    else:
+        gathered = lax.all_gather(child_panels, "row", axis=1, tiled=True)
     blocks = gathered.reshape(children, KMAX, B, WJ)
     blocks = jnp.where(active_columns[:, None, None, :], blocks, jnp.zeros_like(blocks))
     panel_rows = expand_rows(place_bf, blocks)
@@ -52,12 +59,18 @@
     product_table = product.reshape(local_rows, children, WJ)
     own_blocks = local_rows // B
     own_table = lax.dynamic_slice_in_dim(place_bf, row_positions * own_blocks, own_blocks, 2)
-    own_rows = expand_rows(own_table, blocks).reshape(local_rows, children, WJ).astype(jnp.float32)
+    own_rows = expand_rows(own_table, blocks).reshape(local_rows, children, WJ)
+    product_top = lax.reduce_precision(product_table, exponent_bits=8, mantissa_bits=7)
+    product_hi = product_top.astype(jnp.bfloat16)
+    product_lo = (product_table - product_top).astype(jnp.bfloat16)
     partial_value = jnp.einsum(
-        "nca,ncb->cab", own_rows, product_table, precision=lax.Precision.HIGHEST
-    )
+        "nca,ncb->cab", own_rows, product_hi, preferred_element_type=jnp.float32
+    ) + jnp.einsum("nca,ncb->cab", own_rows, product_lo, preferred_element_type=jnp.float32)
     shared_rows = WJ // row_devices
-    reduced_total = lax.psum(partial_value, "row")
+    if row_devices == 2:
+        reduced_total = partial_value + lax.ppermute(partial_value, "row", [(0, 1), (1, 0)])
+    else:
+        reduced_total = lax.psum(partial_value, "row")
     reduced_total = lax.dynamic_slice_in_dim(
         reduced_total, row_positions * shared_rows, shared_rows, 1
     )

time: 928 us -> 906 us (0.976)
  waiting for transfers between devices: 714 us -> 690 us
    all_gather x1 -> x0, waiting for transfers between devices: 17.4 us -> none  [body(): gathered = lax.all_gather(child_panels, 'row', axis=1, tiled=True)]
  transfers between devices with their start and end apart: 3 -> 3, of which waited for: 3 -> 2; matrix products, arithmetic and copies ran while one was open for 6% -> 6% of each run, Pallas kernels for 0% -> 0%
where the time goes in v4:
time: 906 us
  waiting for transfers between devices  690 us (76%)
  matrix products  147 us (16%)
  local copies, waits for them, and re-layouts  36.6 us (4%)
  other arithmetic  17.8 us (2%)
  between operations  14.1 us (2%)
    all_gather x1, waiting for transfers between devices, body(): lax.all_gather(ancestor_sigma, 'snode', axis=1, tiled=True)  687 us
    dot_general x1, matrix products, body(): jnp.dot(lax.all_gather(ancestor_sigma, 'snode', axis=1, tiled=True), pane...  118 us
    convert_element_type x2, local copies, waits for them, and re-layouts, expand_rows(): spread.astype(jnp.bfloat16).reshape(place_table.shape[2] * B, children * WJ)  23.8 us
  transfers between devices with their start and end apart: 3, of which 2 were waited for; matrix products, arithmetic and copies ran while one was open for 6% of the time, Pallas kernels for 0%

profile of v4, /device:TPU:0, one launch (start us, length us, event | category | flops | bytes accessed | tf_op | source)
XLA Modules:
  0.0 905.7 jit_solution(863799635577001834)
XLA Ops:
  7.2 0.7 all-gather.2.cloned.1.call-update
  7.9 0.5 collective-permute-start
  8.4 1.0 select_reduce_fusion
  9.4 0.7 iota_compare_fusion.2
  10.1 0.1 convert_reduce_fusion
  10.3 0.1 dynamic-slice_bitcast_fusion
  10.3 0.1 broadcast_bitcast_fusion
  10.5 0.7 fusion.21
  11.2 0.1 constant_dynamic-slice_fusion
  11.3 2.7 collective-permute-done
  14.1 2.3 broadcast_select_fusion.1
  16.4 0.4 pad_maximum_fusion
  16.8 4.0 convert_bitcast_fusion.1
  20.7 5.8 copy.27
  26.5 7.1 convert_bitcast_fusion
  33.6 18.0 %copy.25 = bf16[64,128,6,128]{1,0,3,2:T(8,128)(2,1)} copy(bf16[64,128,6,128]{3,0,1,2:T(8,128)(2,1)} %convert_bitcast_fusion) | data formatting | bytes 25165824 | tf_op jit(solution)/shard_map/convert_element_type | solution.py:25
  51.6 686.5 %all-gather.2.cloned.1.call-done = bf16[4096,8192]{1,0:T(8,128)(2,1)} async-done(((bf16[4096,512]{1,0:T(8,128)(2,1)}), bf16[4096,8192]{1,0:T(8,128)(2,1)}) %all-gather.2.cloned.1.call-update) | async-done | bytes 67108880 | tf_op jit(solution)/shard_map/all_gather | solution.py:55
  738.1 117.5 %fusion.1 = f32[768,4096]{1,0:T(8,128)} fusion(bf16[4096,8192]{1,0:T(8,128)(2,1)} %all-gather.2.cloned.1.call-done, bf16[96,8,64,128]{3,2,1,0:T(8,128)(2,1)} %bitcast.42), kind=kOutput, calls=%fused_computation.3 | convolution fusion | flops 51539607552 | bytes 92274688 | tf_op jit(solution)/shard_map/dot_general | solution.py:54
  855.6 12.6 %copy.26 = f32[4096,6,128]{2,0,1:T(8,128)} copy(f32[4096,6,128]{0,2,1:T(8,128)} %bitcast.43) | data formatting | bytes 25165824 | tf_op jit(solution)/shard_map/reshape | solution.py:59
  868.2 9.2 %fusion.4 = f32[6,128,128]{2,1,0:T(8,128)S(1)} fusion(bf16[4096,6,128]{2,0,1:T(8,128)(2,1)} %bitcast.38, f32[4096,6,128]{2,0,1:T(8,128)} %copy.26), kind=kOutput, calls=%fused_computation.8 | convolution fusion | flops 814743552 | bytes 19267584 | tf_op jit(solution)/shard_map/nca,ncb->cab/dot_general | solution.py:68
  877.4 8.8 fusion.10
  886.2 0.1 collective-permute-start.1
  886.3 11.7 %multiply_multiply_fusion = f32[4096,6,128]{2,0,1:T(8,128)} fusion(f32[4096,6,128]{2,0,1:T(8,128)} %copy.26, f32[6,128]{1,0:T(8,128)S(1)} %get-tuple-element.4, f32[4096,6]{0,1:T(8,128)S(1)} %bitcast.44), kind=kLoop, calls=%fused_computation.6 | loop fusion | flops 9437184 | bytes 25267200 | tf_op jit(solution)/shard_map/mul | solution.py:89
  898.0 0.8 fusion.13
  (8 shorter events, 0.2 us)
Async XLA Ops:
  7.2 6.9 copy-start
  7.2 730.9 %all-gather.2.cloned.1.call-start = ((), (), s32[]{:S(2)}) async-start(), calls=%async_computation | async-start | bytes 71303168 | tf_op jit(solution)/shard_map/all_gather | solution.py:55
  7.9 6.1 collective-permute-start
  886.2 11.8 %collective-permute-start.1 = (f32[6,128,128]{2,1,0:T(8,128)S(1)}, f32[6,128,128]{2,1,0:T(8,128)S(1)}, u32[]{:S(2)}, u32[]{:S(2)}) collective-permute-start(f32[6,128,128]{2,1,0:T(8,128)S(1)} %fusion.10), channel_id=1, source_target_pairs={{0,1},{1,0},{2,3},{3,2},{4,5},{5,4},{6,7},{7,6},{8,9},{9,8},{10,11... | collective-permute-start | bytes 1179656 | tf_op jit(solution)/shard_map/ppermute | solution.py:71
  886.3 11.7 %copy-start.1 = (f32[6,64,128]{2,1,0:T(8,128)S(1)}, f32[6,64,128]{2,1,0:T(8,128)}, u32[]{:S(2)}) copy-start(f32[6,64,128]{2,1,0:T(8,128)} %param.9) | copy-start | bytes 589828
Sparse Core Ops, SparseCore 0:
  10.8 727.2 all-gather.1

commit v5 on v4

--- a/solution.py
+++ b/solution.py
@@ -51,21 +51,17 @@
     blocks = gathered.reshape(children, KMAX, B, WJ)
     blocks = jnp.where(active_columns[:, None, None, :], blocks, jnp.zeros_like(blocks))
     panel_rows = expand_rows(place_bf, blocks)
-    product = jnp.dot(
-        lax.all_gather(ancestor_sigma, "snode", axis=1, tiled=True),
-        panel_rows,
-        preferred_element_type=jnp.float32,
+    flipped = lax.all_gather(ancestor_sigma.T, "snode", axis=0, tiled=True)
+    product = lax.dot_general(
+        flipped, panel_rows, (((0,), (0,)), ((), ())), preferred_element_type=jnp.float32
     )
     product_table = product.reshape(local_rows, children, WJ)
     own_blocks = local_rows // B
     own_table = lax.dynamic_slice_in_dim(place_bf, row_positions * own_blocks, own_blocks, 2)
     own_rows = expand_rows(own_table, blocks).reshape(local_rows, children, WJ)
-    product_top = lax.reduce_precision(product_table, exponent_bits=8, mantissa_bits=7)
-    product_hi = product_top.astype(jnp.bfloat16)
-    product_lo = (product_table - product_top).astype(jnp.bfloat16)
     partial_value = jnp.einsum(
-        "nca,ncb->cab", own_rows, product_hi, preferred_element_type=jnp.float32
-    ) + jnp.einsum("nca,ncb->cab", own_rows, product_lo, preferred_element_type=jnp.float32)
+        "nca,ncb->cab", own_rows.astype(jnp.float32), product_table, precision=lax.Precision.HIGHEST
+    )
     shared_rows = WJ // row_devices
     if row_devices == 2:
         reduced_total = partial_value + lax.ppermute(partial_value, "row", [(0, 1), (1, 0)])

time: 906 us -> 900 us (level)
    dot_general x3 -> x2, matrix products: 136 us -> 129 us  [the longest x1 118 us: body(): lax.dot_general(flipped, panel_rows, (((0,), (0,)), ((), ())), preferred_...]
where the time goes in v5:
time: 900 us; the launch traced here: 899 us
  waiting for transfers between devices  690 us (77%)
  matrix products  140 us (16%)
  local copies, waits for them, and re-layouts  36.6 us (4%)
  other arithmetic  17.8 us (2%)
  between operations  14.1 us (2%)
    all_gather x1, waiting for transfers between devices, body(): flipped = lax.all_gather(ancestor_sigma.T, 'snode', axis=0, tiled=True)  687 us
    dot_general x1, matrix products, body(): lax.dot_general(flipped, panel_rows, (((0,), (0,)), ((), ())), preferred_...  118 us
    convert_element_type x2, local copies, waits for them, and re-layouts, expand_rows(): spread.astype(jnp.bfloat16).reshape(place_table.shape[2] * B, children * WJ)  23.8 us
  transfers between devices with their start and end apart: 3, of which 2 were waited for; matrix products, arithmetic and copies ran while one was open for 6% of the time, Pallas kernels for 0%

profile of v5, /device:TPU:0, one launch (start us, length us, event | category | flops | bytes accessed | tf_op | source)
XLA Modules:
  0.0 898.7 jit_solution(4280391396216717396)
XLA Ops:
  7.2 0.7 all-gather.2.cloned.1.call-update
  7.9 0.5 collective-permute-start
  8.4 1.0 select_reduce_fusion
  9.4 0.7 iota_compare_fusion.2
  10.1 0.1 convert_reduce_fusion
  10.3 0.1 dynamic-slice_bitcast_fusion
  10.3 0.1 broadcast_bitcast_fusion
  10.4 0.1 copy.45
  10.5 0.7 fusion.16
  11.2 0.1 constant_dynamic-slice_fusion
  11.3 2.7 collective-permute-done
  14.1 2.3 broadcast_select_fusion.1
  16.4 0.4 pad_maximum_fusion
  16.8 4.0 convert_bitcast_fusion.1
  20.7 5.8 copy.24
  26.5 7.1 convert_bitcast_fusion
  33.6 18.0 %copy.22 = bf16[64,128,6,128]{1,0,3,2:T(8,128)(2,1)} copy(bf16[64,128,6,128]{3,0,1,2:T(8,128)(2,1)} %convert_bitcast_fusion) | data formatting | bytes 25165824 | tf_op jit(solution)/shard_map/convert_element_type | solution.py:25
  51.6 686.5 %all-gather.2.cloned.1.call-done = bf16[8192,4096]{0,1:T(8,128)(2,1)} async-done(((bf16[512,4096]{0,1:T(8,128)(2,1)}), bf16[8192,4096]{0,1:T(8,128)(2,1)}) %all-gather.2.cloned.1.call-update) | async-done | bytes 67108880 | tf_op jit(solution)/shard_map/all_gather | solution.py:54
  738.1 117.5 %fusion = f32[768,4096]{1,0:T(8,128)} fusion(bf16[8192,4096]{0,1:T(8,128)(2,1)} %all-gather.2.cloned.1.call-done, bf16[96,8,64,128]{3,2,1,0:T(8,128)(2,1)} %bitcast.44), kind=kOutput, calls=%fused_computation | convolution fusion | flops 51539607552 | bytes 92274688 | tf_op jit(solution)/shard_map/dot_general | solution.py:55
  855.6 12.6 %copy.23 = f32[4096,6,128]{2,0,1:T(8,128)} copy(f32[4096,6,128]{0,2,1:T(8,128)} %bitcast.39) | data formatting | bytes 25165824 | tf_op jit(solution)/shard_map/reshape | solution.py:58
  868.2 11.1 %fusion.18 = f32[6,128,128]{2,1,0:T(8,128)S(1)} fusion(bf16[4096,6,128]{2,0,1:T(8,128)(2,1)} %bitcast.43, f32[4096,6,128]{0,2,1:T(8,128)} %bitcast.40), kind=kOutput, calls=%fused_computation.35 | convolution fusion | flops 4831838208 | bytes 19267584 | tf_op jit(solution)/shard_map/nca,ncb->cab/dot_general | solution.py:62
  879.3 0.1 collective-permute-start.1
  879.4 11.7 %multiply_multiply_fusion = f32[4096,6,128]{2,0,1:T(8,128)} fusion(f32[4096,6,128]{2,0,1:T(8,128)} %copy.23, f32[6,128]{1,0:T(8,128)S(1)} %get-tuple-element.4, f32[4096,6]{0,1:T(8,128)S(1)} %bitcast.46), kind=kLoop, calls=%fused_computation.3 | loop fusion | flops 9437184 | bytes 25267200 | tf_op jit(solution)/shard_map/mul | solution.py:85
  891.1 0.8 fusion.8
  (7 shorter events, 0.1 us)
Async XLA Ops:
  7.2 6.9 copy-start
  7.2 730.9 %all-gather.2.cloned.1.call-start = ((), (), s32[]{:S(2)}) async-start(), calls=%async_computation | async-start | bytes 71303168 | tf_op jit(solution)/shard_map/all_gather | solution.py:54
  7.9 6.1 collective-permute-start
  879.3 11.8 %collective-permute-start.1 = (f32[6,128,128]{2,1,0:T(8,128)S(1)}, f32[6,128,128]{2,1,0:T(8,128)S(1)}, u32[]{:S(2)}, u32[]{:S(2)}) collective-permute-start(f32[6,128,128]{2,1,0:T(8,128)S(1)} %fusion.18), channel_id=1, source_target_pairs={{0,1},{1,0},{2,3},{3,2},{4,5},{5,4},{6,7},{7,6},{8,9},{9,8},{10,11... | collective-permute-start | bytes 1179656 | tf_op jit(solution)/shard_map/ppermute | solution.py:67
  879.4 11.7 %copy-start.1 = (f32[6,64,128]{2,1,0:T(8,128)S(1)}, f32[6,64,128]{2,1,0:T(8,128)}, u32[]{:S(2)}) copy-start(f32[6,64,128]{2,1,0:T(8,128)} %param.9) | copy-start | bytes 589828
Sparse Core Ops, SparseCore 0:
  10.8 727.2 all-gather.1

commit v6 on v5

--- a/solution.py
+++ b/solution.py
@@ -1,3 +1,4 @@
+import numpy as np
 import jax
 import jax.numpy as jnp
 from jax import lax
@@ -23,6 +24,36 @@
     children = blocks.shape[0]
     spread = jnp.einsum("ckn,ckbj->nbcj", place_table, blocks, preferred_element_type=jnp.float32)
     return spread.astype(jnp.bfloat16).reshape(place_table.shape[2] * B, children * WJ)
+
+
+def symmetric_rows(ancestor_sigma, row_position, snode_position, snode_devices):
+    width = ancestor_sigma.shape[1]
+    half = snode_devices // 2
+    quarter = half // 2
+    blocks = ancestor_sigma.reshape(half, width, width)
+    chip_local = snode_position % half
+    shift = jnp.where(snode_position // half == row_position, 0, row_position)
+    pick = (chip_local + shift + jnp.arange(quarter + 1)) % half
+    gathered = lax.all_gather(jnp.take(blocks, pick, axis=0), "snode", axis=0)
+    own = lax.dynamic_slice_in_dim(gathered, row_position * half, half, 0)
+    other = lax.dynamic_slice_in_dim(gathered, (1 - row_position) * half, half, 0)
+    partner = lax.ppermute(other[:, :quarter], "row", [(0, 1), (1, 0)])
+
+    u = np.arange(half)[:, None] + np.zeros((1, half), np.int64)
+    t = np.arange(half)[None, :] + np.zeros((half, 1), np.int64)
+    d = (u - t) % half
+    direct = d <= quarter
+    near = own[np.where(direct, t, u), np.where(direct, d, half - d)]
+    near = jnp.where(direct[:, :, None, None], near, jnp.swapaxes(near, -1, -2))
+    near = near.transpose(0, 2, 1, 3).reshape(half * width, half * width)
+
+    e = (u - t - row_position) % half
+    straight = e < quarter
+    far_a = other[t, jnp.where(straight, e, 0)]
+    far_b = partner[u, jnp.where(straight, 0, half - 1 - e)]
+    far = jnp.where(straight[:, :, None, None], far_a, jnp.swapaxes(far_b, -1, -2))
+    far = far.transpose(0, 2, 1, 3).reshape(half * width, half * width)
+    return near, far
 
 
 def body(
@@ -51,10 +82,26 @@
     blocks = gathered.reshape(children, KMAX, B, WJ)
     blocks = jnp.where(active_columns[:, None, None, :], blocks, jnp.zeros_like(blocks))
     panel_rows = expand_rows(place_bf, blocks)
-    flipped = lax.all_gather(ancestor_sigma.T, "snode", axis=0, tiled=True)
-    product = lax.dot_general(
-        flipped, panel_rows, (((0,), (0,)), ((), ())), preferred_element_type=jnp.float32
-    )
+    snode_devices = lax.axis_size("snode")
+    width = ancestor_sigma.shape[1]
+    if row_devices == 2 and snode_devices % 4 == 0 and local_rows == width * snode_devices // 2:
+        near, far = symmetric_rows(
+            ancestor_sigma, row_positions, lax.axis_index("snode"), snode_devices
+        )
+        product = jnp.dot(
+            near,
+            lax.dynamic_slice_in_dim(panel_rows, row_positions * local_rows, local_rows, 0),
+            preferred_element_type=jnp.float32,
+        ) + jnp.dot(
+            far,
+            lax.dynamic_slice_in_dim(panel_rows, (1 - row_positions) * local_rows, local_rows, 0),
+            preferred_element_type=jnp.float32,
+        )
+    else:
+        flipped = lax.all_gather(ancestor_sigma.T, "snode", axis=0, tiled=True)
+        product = lax.dot_general(
+            flipped, panel_rows, (((0,), (0,)), ((), ())), preferred_element_type=jnp.float32
+        )
     product_table = product.reshape(local_rows, children, WJ)
     own_blocks = local_rows // B
     own_table = lax.dynamic_slice_in_dim(place_bf, row_positions * own_blocks, own_blocks, 2)

time: 900 us -> 990 us (1.10); the launches traced: 899 us -> 978 us
  local copies, waits for them, and re-layouts: 36.6 us -> 355 us
  waiting for transfers between devices: 690 us -> 432 us
  other arithmetic: 17.8 us -> 83.2 us
  matrix products: 140 us -> 92 us
    all_gather x1, waiting for transfers between devices: 687 us -> 432 us  [symmetric_rows(): gathered = lax.all_gather(jnp.take(blocks, pick, axis=0), 'snode', axis=0)]
    gather x0 -> x6, local copies, waits for them, and re-layouts: none -> 145 us  [the longest x2 62 us: symmetric_rows(): near = own[np.where(direct, t, u), np.where(direct, d, half - d)]]
    select_n x0 -> x4, other arithmetic: none -> 66.8 us  [the longest x1 32.5 us: symmetric_rows(): jnp.where(straight[:, :, None, None], far_a, jnp.swapaxes(far_b, -1, -2))]
    unnamed x6 -> x47, local copies, waits for them, and re-layouts: 0.16 us -> 64.9 us
    select_n x0 -> x2, local copies, waits for them, and re-layouts: none -> 62.6 us  [the longest x1 31.4 us: symmetric_rows(): jnp.where(straight[:, :, None, None], far_a, jnp.swapaxes(far_b, -1, -2))]
    dot_general x1 -> x2, matrix products: 118 us -> 68 us  [the longest x1 34.5 us: body(): jnp.dot(far, lax.dynamic_slice_in_dim(panel_rows, (1 - row_positions) * l...]
    dynamic_slice x0 -> x1, local copies, waits for them, and re-layouts: none -> 28.4 us  [symmetric_rows(): lax.dynamic_slice_in_dim(gathered, (1 - row_position) * half, half, 0)]
    slice x0 -> x1, local copies, waits for them, and re-layouts: none -> 13.8 us  [symmetric_rows(): partner = lax.ppermute(other[:, :quarter], 'row', [(0, 1), (1, 0)])]
  transfers between devices with their start and end apart: 3 -> 4, of which waited for: 2 -> 1; matrix products, arithmetic and copies ran while one was open for 6% -> 32% of each run, Pallas kernels for 0% -> 0%
where the time goes in v6:
time: 990 us; the launch traced here: 978 us
  waiting for transfers between devices  432 us (44%)
  local copies, waits for them, and re-layouts  355 us (36%)
  matrix products  92 us (9%)
  other arithmetic  83.2 us (8%)
  between operations  14.7 us (1%)
    all_gather x1, waiting for transfers between devices, symmetric_rows(): gathered = lax.all_gather(jnp.take(blocks, pick, axis=0), 'snode', axis=0)  432 us
    unnamed x47, local copies, waits for them, and re-layouts  64.9 us
    gather x2, local copies, waits for them, and re-layouts, symmetric_rows(): near = own[np.where(direct, t, u), np.where(direct, d, half - d)]  62 us
    gather x2, local copies, waits for them, and re-layouts, symmetric_rows(): far_b = partner[u, jnp.where(straight, 0, half - 1 - e)]  60.8 us
    dot_general x1, matrix products, body(): jnp.dot(far, lax.dynamic_slice_in_dim(panel_rows, (1 - row_positions) * l...  34.5 us
    dot_general x1, matrix products, body(): jnp.dot(near, lax.dynamic_slice_in_dim(panel_rows, row_positions * local_...  33.5 us
    select_n x1, other arithmetic, symmetric_rows(): jnp.where(straight[:, :, None, None], far_a, jnp.swapaxes(far_b, -1, -2))  32.5 us
    select_n x1, other arithmetic, symmetric_rows(): near = jnp.where(direct[:, :, None, None], near, jnp.swapaxes(near, -1, -2))  32.5 us
  transfers between devices with their start and end apart: 4, of which 1 were waited for; matrix products, arithmetic and copies ran while one was open for 32% of the time, Pallas kernels for 0%

profile of v6, /device:TPU:0, one launch (start us, length us, event | category | flops | bytes accessed | tf_op | source)
XLA Modules:
  0.0 978.4 jit_solution(12213026283134619561)
XLA Ops:
  12.6 432.3 %all-gather.2.cloned.1.call-done = bf16[16,5,512,512]{3,2,1,0:T(8,128)(2,1)} async-done(((bf16[1,5,512,512]{3,2,1,0:T(8,128)(2,1)}), bf16[16,5,512,512]{3,2,1,0:T(8,128)(2,1)}) %all-gather.2.cloned.1.call-update) | async-done | bytes 41943056 | tf_op jit(solution)/shard_map/all_gather | solution.py:37
  444.9 13.8 %constant_dynamic-slice_fusion.2 = bf16[8,4,512,512]{3,2,1,0:T(8,128)(2,1)} fusion(bf16[16,5,512,512]{3,2,1,0:T(8,128)(2,1)} %all-gather.2.cloned.1.call-done, s32[]{:T(128)S(6)} %select_n.160), kind=kLoop, calls=%fused_computation.61 | loop fusion | bytes 33554436 | tf_op jit(solution)/shard_map/slice | solution.py:40
  468.0 7.1 convert_bitcast_fusion
  475.1 18.1 %copy.59 = bf16[64,128,6,128]{1,0,3,2:T(8,128)(2,1)} copy(bf16[64,128,6,128]{3,0,1,2:T(8,128)(2,1)} %convert_bitcast_fusion) | data formatting | bytes 25165824 | tf_op jit(solution)/shard_map/convert_element_type | solution.py:26
  493.1 16.0 %copy.83 = bf16[96,8,64,128]{3,1,2,0:T(8,128)(2,1)} copy(bf16[96,8,64,128]{3,2,1,0:T(8,128)(2,1)} %bitcast.67) | data formatting | bytes 25165824
  509.1 5.6 convert_bitcast_fusion.1
  514.7 7.9 copy.63
  522.5 28.4 %constant_dynamic-slice_fusion.1 = (bf16[8,5,512,512]{3,2,1,0:T(8,128)(2,1)}, bf16[8,5,512,512]{3,2,1,0:T(8,128)(2,1)}) fusion(bf16[16,5,512,512]{3,2,1,0:T(8,128)(2,1)} %all-gather.2.cloned.1.call-done, s32[]{:T(128)S(6)} %select_n.160, s32[]{:T(128)S(6)} %select_n.149), kind=kLoop, calls=%fused_computation.59 | loop fusion | bytes 83886088 | tf_op jit(solution)/shard_map/dynamic_slice | solution.py:39
  551.0 19.7 %gather_fusion.1 = bf16[64,512,512]{2,1,0:T(8,128)(2,1)} fusion(bf16[8,5,512,512]{3,2,1,0:T(8,128)(2,1)} %get-tuple-element.3, s32[64]{0:T(128)S(1)} %copy-done.4), kind=kCustom, calls=%fused_computation.1 | custom fusion | bytes 67109376 | tf_op jit(solution)/shard_map/gather | solution.py:46
  570.7 42.3 %copy.55 = bf16[8,8,512,512]{2,3,1,0:T(8,128)(2,1)} copy(bf16[8,8,512,512]{3,2,1,0:T(8,128)(2,1)} %bitcast.59) | data formatting | bytes 67108864 | tf_op jit(solution)/shard_map/gather | solution.py:46
  612.9 32.5 %bitcast_select_fusion.1 = bf16[8,512,8,512]{3,1,2,0:T(8,128)(2,1)} fusion(bf16[8,512,8,512]{3,1,2,0:T(8,128)(2,1)} %bitcast.60, bf16[8,8,512,512]{2,3,1,0:T(8,128)(2,1)} %copy.55, pred[8,8]{1,0:T(8,128)(4,1)S(1)} %copy-done.15), kind=kLoop, calls=%fused_computation.5 | loop fusion | flops 16777216 | bytes 100663360 | tf_op jit(solution)/shard_map/jit(_where)/select_n | solution.py:47
  645.4 31.2 %copy.56 = bf16[8,512,8,512]{3,2,1,0:T(8,128)(2,1)} copy(bf16[8,512,8,512]{3,1,2,0:T(8,128)(2,1)} %bitcast_select_fusion.1) | data formatting | bytes 67108864 | tf_op jit(solution)/shard_map/jit(_where)/select_n | solution.py:47
  676.6 22.7 %copy.72 = bf16[512,8,8,512]{3,1,2,0:T(8,128)(2,1)} copy(bf16[512,8,8,512]{3,2,1,0:T(8,128)(2,1)} %bitcast.63) | data formatting | bytes 67108864
  699.4 19.2 %gather_fusion.2 = bf16[64,512,512]{2,1,0:T(8,128)(2,1)} fusion(bf16[8,5,512,512]{3,2,1,0:T(8,128)(2,1)} %get-tuple-element.2, s32[64]{0:T(128)S(1)} %copy-done.3), kind=kCustom, calls=%fused_computation.2 | custom fusion | bytes 67109376 | tf_op jit(solution)/shard_map/gather | solution.py:52
  718.6 33.5 %fusion.1 = f32[4096,768]{0,1:T(8,128)} fusion(bf16[4096,4096]{1,0:T(8,128)(2,1)} %bitcast.72, bf16[8192,768]{0,1:T(8,128)(2,1)} %bitcast.75, s32[]{:T(128)S(6)} %select_n.158), kind=kOutput, calls=%fused_computation.14 | convolution fusion | flops 25769803776 | bytes 52428804 | tf_op jit(solution)/shard_map/dot_general | solution.py:91
  752.1 18.5 %gather_fusion.3 = bf16[64,512,512]{2,1,0:T(8,128)(2,1)} fusion(bf16[8,4,512,512]{3,2,1,0:T(8,128)(2,1)} %collective-permute-done.1, s32[64]{0:T(128)S(1)} %copy-done.2), kind=kCustom, calls=%fused_computation.3 | custom fusion | bytes 67109376 | tf_op jit(solution)/shard_map/gather | solution.py:53
  770.6 42.3 %copy.60 = bf16[8,8,512,512]{2,3,1,0:T(8,128)(2,1)} copy(bf16[8,8,512,512]{3,2,1,0:T(8,128)(2,1)} %bitcast.62) | data formatting | bytes 67108864 | tf_op jit(solution)/shard_map/gather | solution.py:53
  812.9 32.5 %bitcast_select_fusion = bf16[8,512,8,512]{3,1,2,0:T(8,128)(2,1)} fusion(bf16[8,512,8,512]{3,1,2,0:T(8,128)(2,1)} %bitcast.61, bf16[8,8,512,512]{2,3,1,0:T(8,128)(2,1)} %copy.60, pred[8,8]{1,0:T(8,128)(4,1)S(1)} %copy-done.11), kind=kLoop, calls=%fused_computation.4 | loop fusion | flops 16777216 | bytes 100663360 | tf_op jit(solution)/shard_map/jit(_where)/select_n | solution.py:54
  845.5 31.4 %copy.61 = bf16[8,512,8,512]{3,2,1,0:T(8,128)(2,1)} copy(bf16[8,512,8,512]{3,1,2,0:T(8,128)(2,1)} %bitcast_select_fusion) | data formatting | bytes 67108864 | tf_op jit(solution)/shard_map/jit(_where)/select_n | solution.py:54
  876.9 22.8 %copy.74 = bf16[512,8,8,512]{3,1,2,0:T(8,128)(2,1)} copy(bf16[512,8,8,512]{3,2,1,0:T(8,128)(2,1)} %bitcast.64) | data formatting | bytes 67108864
  899.6 34.5 %convolution_add_fusion = f32[4096,768]{0,1:T(8,128)} fusion(f32[4096,768]{0,1:T(8,128)} %fusion.1, bf16[4096,4096]{1,0:T(8,128)(2,1)} %bitcast.73, bf16[8192,768]{0,1:T(8,128)(2,1)} %bitcast.76, s32[]{:T(128)S(6)} %select_n.168), kind=kOutput, calls=%fused_computation.9 | convolution fusion | flops 25772949504 | bytes 65011716 | tf_op jit(solution)/shard_map/dot_general | solution.py:95
  934.1 12.6 %copy.62 = f32[4096,6,128]{2,0,1:T(8,128)} copy(f32[4096,6,128]{0,2,1:T(8,128)} %bitcast.65) | data formatting | bytes 25165824 | tf_op jit(solution)/shard_map/reshape | solution.py:105
  946.7 11.4 %fusion.30 = f32[6,128,128]{2,1,0:T(8,128)S(1)} fusion(bf16[4096,6,128]{2,0,1:T(8,128)(2,1)} %bitcast.74, f32[4096,6,128]{0,2,1:T(8,128)} %bitcast.66), kind=kOutput, calls=%fused_computation.77 | convolution fusion | flops 4831838208 | bytes 19267584 | tf_op jit(solution)/shard_map/nca,ncb->cab/dot_general | solution.py:109
  958.6 11.7 %multiply_multiply_fusion = f32[4096,6,128]{2,0,1:T(8,128)} fusion(f32[4096,6,128]{2,0,1:T(8,128)} %copy.62, f32[6,128]{1,0:T(8,128)S(1)} %copy-done.8, f32[4096,6]{0,1:T(8,128)S(1)} %bitcast.78), kind=kLoop, calls=%fused_computation.7 | loop fusion | flops 9437184 | bytes 25267200 | tf_op jit(solution)/shard_map/mul | solution.py:132
  (72 shorter events, 16.0 us)
Async XLA Ops:
  7.2 437.8 %all-gather.2.cloned.1.call-start = ((), (), s32[]{:S(2)}) async-start(), calls=%async_computation | async-start | bytes 44564480 | tf_op jit(solution)/shard_map/all_gather | solution.py:37
  12.0 450.6 %collective-permute-start = (bf16[6,2048,128]{2,1,0:T(8,128)(2,1)}, bf16[6,2048,128]{2,1,0:T(8,128)(2,1)}, u32[]{:S(2)}, u32[]{:S(2)}) collective-permute-start(bf16[6,2048,128]{2,1,0:T(8,128)(2,1)} %param.18), channel_id=1, source_target_pairs={{0,1},{1,0},{2,3},{3,2},{4,5},{5,4},{6,7},{7,6},{8,9},{9,8},{10,11... | collective-permute-start | bytes 9437192 | tf_op jit(solution)/shard_map/ppermute | solution.py:75
  12.5 446.2 %copy-start.10 = (s32[8,8]{1,0:T(8,128)S(1)}, s32[8,8]{1,0:T(8,128)}, u32[]{:S(2)}) copy-start(s32[8,8]{1,0:T(8,128)} %constant.108.clone) | copy-start | bytes 772
  12.6 446.2 %copy-start.13 = (s32[8,8]{1,0:T(8,128)S(1)}, s32[8,8]{1,0:T(8,128)}, u32[]{:S(2)}) copy-start(s32[8,8]{1,0:T(8,128)} %constant.173) | copy-start | bytes 772
  12.6 446.2 %copy-start.14 = (s32[8,8]{1,0:T(8,128)S(1)}, s32[8,8]{1,0:T(8,128)}, u32[]{:S(2)}) copy-start(s32[8,8]{1,0:T(8,128)} %constant.174) | copy-start | bytes 772
  12.6 447.4 %copy-start.12 = (s32[6,32]{1,0:T(8,128)S(1)}, s32[6,32]{1,0:T(8,128)}, u32[]{:S(2)}) copy-start(s32[6,32]{1,0:T(8,128)} %param.20) | copy-start | bytes 2308
  12.6 447.4 %copy-start.16 = (s32[64]{0:T(128)S(1)}, s32[64]{0:T(128)}, u32[]{:S(2)}) copy-start(s32[64]{0:T(128)} %param.23) | copy-start | bytes 772
  12.6 447.6 %copy-start.18 = (s32[6]{0:T(128)S(1)}, s32[6]{0:T(128)}, u32[]{:S(2)}) copy-start(s32[6]{0:T(128)} %param.21) | copy-start | bytes 76
  12.6 448.7 %copy-start.17 = (s32[6]{0:T(128)S(1)}, s32[6]{0:T(128)}, u32[]{:S(2)}) copy-start(s32[6]{0:T(128)} %param.22) | copy-start | bytes 76
  12.6 450.1 %copy-start.1 = (bf16[6,2048,128]{2,1,0:T(8,128)(2,1)S(1)}, bf16[6,2048,128]{2,1,0:T(8,128)(2,1)}, u32[]{:S(2)}) copy-start(bf16[6,2048,128]{2,1,0:T(8,128)(2,1)} %param.18) | copy-start | bytes 9437188
  458.7 293.4 %collective-permute-start.1 = (bf16[8,4,512,512]{3,2,1,0:T(8,128)(2,1)}, bf16[8,4,512,512]{3,2,1,0:T(8,128)(2,1)}, u32[]{:S(2)}, u32[]{:S(2)}) collective-permute-start(bf16[8,4,512,512]{3,2,1,0:T(8,128)(2,1)} %constant_dynamic-slice_fusion.2), channel_id=1, source_target_pairs={{0,1},{1,0},{2,3},{3,2},{4,5},{5,4},{6,7},{7,6},{8,9},{9,8},{10,11... | collective-permute-start | bytes 50331656 | tf_op jit(solution)/shard_map/ppermute | solution.py:40
  465.4 2.6 copy-start
  475.1 34.0 %slice-start = ((s8[6291456]{0:T(1024)(128)(4,1)}), s8[2097152]{0:T(1024)(128)(4,1)S(1)}, s32[]{:S(2)}) async-start(s8[6291456]{0:T(1024)(128)(4,1)} %bitcast.69), calls=%async_computation.1 | async-start | bytes 4194304
  493.1 16.0 %slice-start.1 = ((s8[6291456]{0:T(1024)(128)(4,1)}), s8[4194304]{0:T(1024)(128)(4,1)S(1)}, s32[]{:S(2)}) async-start(s8[6291456]{0:T(1024)(128)(4,1)} %bitcast.69), calls=%async_computation.2 | async-start | bytes 8388608
  522.5 28.4 %copy-start.4 = (s32[64]{0:T(128)S(1)}, s32[64]{0:T(128)}, u32[]{:S(2)}) copy-start(s32[64]{0:T(128)} %constant.168) | copy-start | bytes 772
  570.7 42.3 %copy-start.15 = (pred[8,8]{1,0:T(8,128)(4,1)S(1)}, pred[8,8]{1,0:T(8,128)(4,1)}, u32[]{:S(2)}) copy-start(pred[8,8]{1,0:T(8,128)(4,1)} %constant.116) | copy-start | bytes 196
  676.6 22.7 %copy-start.3 = (s32[64]{0:T(128)S(1)}, s32[64]{0:T(128)}, u32[]{:S(2)}) copy-start(s32[64]{0:T(128)} %reshape.180) | copy-start | bytes 772
  718.6 33.5 %copy-start.2 = (s32[64]{0:T(128)S(1)}, s32[64]{0:T(128)}, u32[]{:S(2)}) copy-start(s32[64]{0:T(128)} %reshape.186) | copy-start | bytes 772
  770.6 42.3 %copy-start.11 = (pred[8,8]{1,0:T(8,128)(4,1)S(1)}, pred[8,8]{1,0:T(8,128)(4,1)}, u32[]{:S(2)}) copy-start(pred[8,8]{1,0:T(8,128)(4,1)} %broadcast_compare_fusion) | copy-start | bytes 196
  946.7 11.9 %copy-start.5 = (f32[1,6,32,128]{3,1,2,0:T(8,128)S(1)}, f32[1,6,32,128]{3,1,2,0:T(8,128)}, u32[]{:S(2)}) copy-start(f32[1,6,32,128]{3,1,2,0:T(8,128)} %copy.84) | copy-start | bytes 294916
  946.7 11.9 %copy-start.8 = (f32[6,128]{1,0:T(8,128)S(1)}, f32[6,128]{1,0:T(8,128)}, u32[]{:S(2)}) copy-start(f32[6,128]{1,0:T(8,128)} %copy-done.7) | copy-start | bytes 9220
  958.0 12.3 %collective-permute-start.2 = (f32[6,128,128]{2,1,0:T(8,128)S(1)}, f32[6,128,128]{2,1,0:T(8,128)S(1)}, u32[]{:S(2)}, u32[]{:S(2)}) collective-permute-start(f32[6,128,128]{2,1,0:T(8,128)S(1)} %fusion.30), channel_id=1, source_target_pairs={{0,1},{1,0},{2,3},{3,2},{4,5},{5,4},{6,7},{7,6},{8,9},{9,8},{10,11... | collective-permute-start | bytes 1179656 | tf_op jit(solution)/shard_map/ppermute | solution.py:114
  958.6 11.7 %copy-start.6 = (f32[6,64,128]{2,1,0:T(8,128)S(1)}, f32[6,64,128]{2,1,0:T(8,128)}, u32[]{:S(2)}) copy-start(f32[6,64,128]{2,1,0:T(8,128)} %param.19) | copy-start | bytes 589828
  958.6 11.7 %copy-start.9 = (f32[6,64]{1,0:T(8,128)S(1)}, f32[6,64]{1,0:T(8,128)}, u32[]{:S(2)}) copy-start(f32[6,64]{1,0:T(8,128)} %constant_dynamic-slice_fusion) | copy-start | bytes 4612
  (1 other events, 1.2 us)
Sparse Core Ops, SparseCore 0:
  12.2 432.7 all-gather.1

commit v7 on v5

--- a/solution.py
+++ b/solution.py
@@ -1,6 +1,9 @@
+import numpy as np
 import jax
 import jax.numpy as jnp
 from jax import lax
+from jax.experimental import pallas as pl
+from jax.experimental.pallas import tpu as pltpu
 from jax.sharding import PartitionSpec as P
 
 B = 128
@@ -24,6 +27,74 @@
     spread = jnp.einsum("ckn,ckbj->nbcj", place_table, blocks, preferred_element_type=jnp.float32)
     return spread.astype(jnp.bfloat16).reshape(place_table.shape[2] * B, children * WJ)
 
+
+def block_product_kernel(src_ref, far_ref, pick_ref, flip_ref, pool_ref, swap_ref, rows_ref, out_ref, acc_ref):
+    t = pl.program_id(1)
+    at = pl.program_id(0) * pl.num_programs(1) + t
+
+    @pl.when(t == 0)
+    def _():
+        acc_ref[...] = jnp.zeros_like(acc_ref)
+
+    block = jnp.where(pick_ref[at] == 0, pool_ref[0], swap_ref[0])
+    block = lax.cond(flip_ref[at] == 1, lambda b: b.T, lambda b: b, block)
+    acc_ref[...] += jnp.dot(block, rows_ref[0], preferred_element_type=jnp.float32)
+
+    @pl.when(t == pl.num_programs(1) - 1)
+    def _():
+        out_ref[...] = acc_ref[...]
+
+
+def symmetric_product(ancestor_sigma, panel_rows, row_position, snode_position, snode_devices):
+    width = ancestor_sigma.shape[1]
+    half = snode_devices // 2
+    quarter = half // 2
+    cols = panel_rows.shape[1]
+    blocks = ancestor_sigma.reshape(half, width, width)
+    chip_local = snode_position % half
+    shift = jnp.where(snode_position // half == row_position, 0, row_position)
+    pick = (chip_local + shift + jnp.arange(quarter + 1)) % half
+    gathered = lax.all_gather(jnp.take(blocks, pick, axis=0), "snode", axis=0)
+    other = lax.dynamic_slice_in_dim(gathered, (1 - row_position) * half, half, 0)
+    partner = lax.ppermute(other[:, :quarter], "row", [(0, 1), (1, 0)])
+    pool = gathered.reshape(snode_devices * (quarter + 1), width, width)
+    swap = partner.reshape(half * quarter, width, width)
+
+    u = jnp.arange(half)[:, None]
+    t = jnp.arange(snode_devices)[None, :]
+    near = (t // half) == row_position
+    local = t % half
+    d = (u - local) % half
+    near_src = jnp.where(
+        d <= quarter,
+        (row_position * half + local) * (quarter + 1) + d,
+        (row_position * half + u) * (quarter + 1) + half - d,
+    )
+    e = (u - local - row_position) % half
+    straight = e < quarter
+    far_src = ((1 - row_position) * half + local) * (quarter + 1) + jnp.where(straight, e, 0)
+    src = jnp.where(near, near_src, jnp.where(straight, far_src, 0))
+    far = jnp.where(near | straight, 0, u * quarter + half - 1 - e)
+    pick_swap = jnp.where(near | straight, 0, 1)
+    flip = jnp.where(near, d > quarter, ~straight).astype(jnp.int32)
+    tables = [x.reshape(-1).astype(jnp.int32) for x in (src, far, pick_swap, flip)]
+
+    grid_spec = pltpu.PrefetchScalarGridSpec(
+        num_scalar_prefetch=4,
+        grid=(half, snode_devices),
+        in_specs=[
+            pl.BlockSpec((1, width, width), lambda i, j, s, f, p, q: (s[i * snode_devices + j], 0, 0)),
+            pl.BlockSpec((1, width, width), lambda i, j, s, f, p, q: (f[i * snode_devices + j], 0, 0)),
+            pl.BlockSpec((1, width, cols), lambda i, j, s, f, p, q: (j, 0, 0)),
+        ],
+        out_specs=pl.BlockSpec((width, cols), lambda i, j, s, f, p, q: (i, 0)),
+        scratch_shapes=[pltpu.VMEM((width, cols), jnp.float32)],
+    )
+    return pl.pallas_call(
+        block_product_kernel,
+        grid_spec=grid_spec,
+        out_shape=jax.ShapeDtypeStruct((half * width, cols), jnp.float32),
+    )(*tables, pool, swap, panel_rows.reshape(snode_devices, width, cols))
 
 def body(
     ancestor_sigma,
@@ -51,10 +122,17 @@
     blocks = gathered.reshape(children, KMAX, B, WJ)
     blocks = jnp.where(active_columns[:, None, None, :], blocks, jnp.zeros_like(blocks))
     panel_rows = expand_rows(place_bf, blocks)
-    flipped = lax.all_gather(ancestor_sigma.T, "snode", axis=0, tiled=True)
-    product = lax.dot_general(
-        flipped, panel_rows, (((0,), (0,)), ((), ())), preferred_element_type=jnp.float32
-    )
+    snode_devices = lax.axis_size("snode")
+    width = ancestor_sigma.shape[1]
+    if row_devices == 2 and snode_devices % 4 == 0 and local_rows == width * snode_devices // 2:
+        product = symmetric_product(
+            ancestor_sigma, panel_rows, row_positions, lax.axis_index("snode"), snode_devices
+        )
+    else:
+        flipped = lax.all_gather(ancestor_sigma.T, "snode", axis=0, tiled=True)
+        product = lax.dot_general(
+            flipped, panel_rows, (((0,), (0,)), ((), ())), preferred_element_type=jnp.float32
+        )
     product_table = product.reshape(local_rows, children, WJ)
     own_blocks = local_rows // B
     own_table = lax.dynamic_slice_in_dim(place_bf, row_positions * own_blocks, own_blocks, 2)

time: 900 us -> 746 us (0.83)
  waiting for transfers between devices: 690 us -> 445 us
  Pallas kernels: 0 us -> 149 us
  matrix products: 140 us -> 25.3 us
  local copies, waits for them, and re-layouts: 36.6 us -> 88.2 us
    all_gather x1, waiting for transfers between devices: 687 us -> 433 us  [symmetric_product(): gathered = lax.all_gather(jnp.take(blocks, pick, axis=0), 'snode', axis=0)]
    pallas_call x0 -> x1, Pallas kernels: none -> 149 us  [symmetric_product(): pl.pallas_call(block_product_kernel, grid_spec=grid_spec, out_shape=jax.S...]
    dot_general x1 -> x0, matrix products: 118 us -> none  [body(): lax.dot_general(flipped, panel_rows, (((0,), (0,)), ((), ())), preferred_...]
    another operation x0 -> x2, local copies, waits for them, and re-layouts: none -> 40.2 us  [symmetric_product(): panel_rows.reshape(snode_devices, width, cols)]
    convert_element_type x2 -> x1, local copies, waits for them, and re-layouts: 23.8 us -> 5.2 us  [expand_rows(): spread.astype(jnp.bfloat16).reshape(place_table.shape[2] * B, children * WJ)]
    slice x0 -> x1, local copies, waits for them, and re-layouts: none -> 13.7 us  [symmetric_product(): partner = lax.ppermute(other[:, :quarter], 'row', [(0, 1), (1, 0)])]
    unnamed x6 -> x17, local copies, waits for them, and re-layouts: 0.16 us -> 12.8 us
    pallas_call x0 -> x1, local copies, waits for them, and re-layouts: none -> 12.6 us  [symmetric_product(): pl.pallas_call(block_product_kernel, grid_spec=grid_spec, out_shape=jax.S...]
  transfers between devices with their start and end apart: 3 -> 4, of which waited for: 2 -> 2; matrix products, arithmetic and copies ran while one was open for 6% -> 12% of each run, Pallas kernels for 0% -> 0%
where the time goes in v7:
time: 746 us; the launch traced here: 742 us
  waiting for transfers between devices  445 us (60%)
  Pallas kernels  149 us (20%)
  local copies, waits for them, and re-layouts  88.2 us (12%)
  matrix products  25.3 us (3%)
  other arithmetic  19.1 us (3%)
  between operations  14.3 us (2%)
    all_gather x1, waiting for transfers between devices, symmetric_product(): gathered = lax.all_gather(jnp.take(blocks, pick, axis=0), 'snode', axis=0)  433 us
    pallas_call x1, Pallas kernels, symmetric_product(): pl.pallas_call(block_product_kernel, grid_spec=grid_spec, out_shape=jax.S...  149 us
    another operation x2, local copies, waits for them, and re-layouts, symmetric_product(): panel_rows.reshape(snode_devices, width, cols)  40.2 us
  transfers between devices with their start and end apart: 4, of which 2 were waited for; matrix products, arithmetic and copies ran while one was open for 12% of the time, Pallas kernels for 0%

profile of v7, /device:TPU:0, one launch (start us, length us, event | category | flops | bytes accessed | tf_op | source)
XLA Modules:
  0.0 741.8 jit_solution(13327455695910712774)
XLA Ops:
  7.3 2.9 gather_fusion
  10.2 1.8 bitcast_select_fusion
  12.1 432.8 %all-gather.2.cloned.1.call-done = bf16[16,5,512,512]{3,2,1,0:T(8,128)(2,1)} async-done(((bf16[1,5,512,512]{3,2,1,0:T(8,128)(2,1)}), bf16[16,5,512,512]{3,2,1,0:T(8,128)(2,1)}) %all-gather.2.cloned.1.call-update) | async-done | bytes 41943056 | tf_op jit(solution)/shard_map/all_gather | solution.py:57
  444.9 13.7 %constant_dynamic-slice_fusion.1 = bf16[8,4,512,512]{3,2,1,0:T(8,128)(2,1)} fusion(bf16[16,5,512,512]{3,2,1,0:T(8,128)(2,1)} %all-gather.2.cloned.1.call-done, s32[]{:T(128)S(6)} %select_n.204), kind=kLoop, calls=%fused_computation.52 | loop fusion | bytes 33554436 | tf_op jit(solution)/shard_map/slice | solution.py:59
  458.7 0.5 collective-permute-start.1
  459.9 0.3 select_reduce_fusion
  460.2 0.1 convert_reduce_fusion
  460.8 0.5 select_convert_fusion
  461.3 0.6 broadcast_select_fusion.2
  461.9 11.7 %collective-permute-done.1 = bf16[6,2048,128]{2,1,0:T(8,128)(2,1)} collective-permute-done((bf16[6,2048,128]{2,1,0:T(8,128)(2,1)S(1)}, bf16[6,2048,128]{2,1,0:T(8,128)(2,1)}, u32[]{:S(2)}, u32[]{:S(2)}) %collective-permute-start.1) | collective-permute-done | bytes 3145760 | tf_op jit(solution)/shard_map/ppermute | solution.py:115
  473.7 2.3 broadcast_select_fusion.1
  476.0 0.4 pad_maximum_fusion
  476.4 7.1 convert_bitcast_fusion
  483.5 13.7 %copy.47 = bf16[64,128,6,128]{3,2,1,0:T(8,128)(2,1)} copy(bf16[64,128,6,128]{3,0,1,2:T(8,128)(2,1)} %convert_bitcast_fusion) | data formatting | bytes 25165824 | tf_op jit(solution)/shard_map/reshape;reshape | solution.py:97
  497.2 26.5 %reshape.273.rows_ref = bf16[16,512,768]{2,1,0:T(8,128)(2,1)} reshape(bf16[64,128,6,128]{3,2,1,0:T(8,128)(2,1)} %copy.47) | data formatting | bytes 25165824 | tf_op jit(solution)/shard_map/reshape;reshape | solution.py:97
  523.7 7.1 convert_bitcast_fusion.1
  530.8 5.2 copy.37
  536.0 149.3 %shard_map.86 = f32[4096,768]{1,0:T(8,128)} custom-call(s32[128]{0:T(128)} %get-tuple-element.14.src_ref, s32[128]{0:T(128)} %get-tuple-element.13.far_ref, s32[128]{0:T(128)} %get-tuple-element.12.pick_ref, s32[128]{0:T(128)} %get-tuple-element.8.flip_ref, bf16[80,512,512]{2,1,0:T(8,128)(2,1)} %bitcast.37, bf16[32,512,512]{2,1,0:T(8,128)(2,1)} %bitcast.4.swap_ref, ...), custom_call_target="tpu_custom_call" | custom-call | tf_op jit(solution)/shard_map/pallas_call | solution.py:93
  685.3 12.6 %copy.36 = f32[4096,768]{0,1:T(8,128)} copy(f32[4096,768]{1,0:T(8,128)} %shard_map.86) | data formatting | bytes 25165824 | tf_op jit(solution)/shard_map/pallas_call | solution.py:93
  697.9 11.1 %fusion.22 = f32[6,128,128]{2,1,0:T(8,128)S(1)} fusion(bf16[4096,6,128]{2,0,1:T(8,128)(2,1)} %bitcast.40, f32[4096,6,128]{0,2,1:T(8,128)} %bitcast.35), kind=kOutput, calls=%fused_computation.73 | convolution fusion | flops 4831838208 | bytes 19267584 | tf_op jit(solution)/shard_map/nca,ncb->cab/dot_general | solution.py:140
  709.0 0.5 collective-permute-start.2
  709.5 12.0 %multiply_multiply_fusion = f32[4096,6,128]{0,2,1:T(8,128)} fusion(f32[4096,6,128]{0,2,1:T(8,128)} %bitcast.36, f32[6,128]{1,0:T(8,128)S(1)} %get-tuple-element.15, f32[4096,6]{0,1:T(8,128)S(1)} %bitcast.42), kind=kLoop, calls=%fused_computation.1 | loop fusion | flops 9437184 | bytes 25267200 | tf_op jit(solution)/shard_map/mul | solution.py:163
  721.5 12.6 %copy.40 = f32[4096,6,128]{2,0,1:T(8,128)} copy(f32[4096,6,128]{0,2,1:T(8,128)} %multiply_multiply_fusion) | data formatting | bytes 25165824
  734.2 0.8 fusion.5
  (46 shorter events, 1.3 us)
Async XLA Ops:
  7.2 437.8 %all-gather.2.cloned.1.call-start = ((), (), s32[]{:S(2)}) async-start(), calls=%async_computation | async-start | bytes 44564480 | tf_op jit(solution)/shard_map/all_gather | solution.py:57
  12.0 446.6 %copy-start.1 = (bf16[6,2048,128]{2,1,0:T(8,128)(2,1)S(1)}, bf16[6,2048,128]{2,1,0:T(8,128)(2,1)}, u32[]{:S(2)}) copy-start(bf16[6,2048,128]{2,1,0:T(8,128)(2,1)} %param.8) | copy-start | bytes 9437188
  12.0 447.8 %copy-start.3 = (s32[6,32]{1,0:T(8,128)S(1)}, s32[6,32]{1,0:T(8,128)}, u32[]{:S(2)}) copy-start(s32[6,32]{1,0:T(8,128)} %param.10) | copy-start | bytes 2308
  12.1 447.8 %copy-start.4 = (s32[64]{0:T(128)S(1)}, s32[64]{0:T(128)}, u32[]{:S(2)}) copy-start(s32[64]{0:T(128)} %param.13) | copy-start | bytes 772
  12.1 448.1 %copy-start.6 = (s32[6]{0:T(128)S(1)}, s32[6]{0:T(128)}, u32[]{:S(2)}) copy-start(s32[6]{0:T(128)} %param.11) | copy-start | bytes 76
  12.1 448.5 %copy-start.5 = (s32[6]{0:T(128)S(1)}, s32[6]{0:T(128)}, u32[]{:S(2)}) copy-start(s32[6]{0:T(128)} %param.12) | copy-start | bytes 76
  458.7 77.4 %collective-permute-start = (bf16[8,4,512,512]{3,2,1,0:T(8,128)(2,1)}, bf16[8,4,512,512]{3,2,1,0:T(8,128)(2,1)}, u32[]{:S(2)}, u32[]{:S(2)}) collective-permute-start(bf16[8,4,512,512]{3,2,1,0:T(8,128)(2,1)} %constant_dynamic-slice_fusion.1), channel_id=1, source_target_pairs={{0,1},{1,0},{2,3},{3,2},{4,5},{5,4},{6,7},{7,6},{8,9},{9,8},{10,11... | collective-permute-start | bytes 50331656 | tf_op jit(solution)/shard_map/ppermute | solution.py:59
  458.7 15.0 %collective-permute-start.1 = (bf16[6,2048,128]{2,1,0:T(8,128)(2,1)S(1)}, bf16[6,2048,128]{2,1,0:T(8,128)(2,1)}, u32[]{:S(2)}, u32[]{:S(2)}) collective-permute-start(bf16[6,2048,128]{2,1,0:T(8,128)(2,1)S(1)} %copy-done.1), channel_id=1, source_target_pairs={{0,1},{1,0},{2,3},{3,2},{4,5},{5,4},{6,7},{7,6},{8,9},{9,8},{10,11... | collective-permute-start | bytes 9437192 | tf_op jit(solution)/shard_map/ppermute | solution.py:115
  476.4 7.1 copy-start
  709.0 25.2 %collective-permute-start.2 = (f32[6,128,128]{2,1,0:T(8,128)S(1)}, f32[6,128,128]{2,1,0:T(8,128)S(1)}, u32[]{:S(2)}, u32[]{:S(2)}) collective-permute-start(f32[6,128,128]{2,1,0:T(8,128)S(1)} %fusion.22), channel_id=1, source_target_pairs={{0,1},{1,0},{2,3},{3,2},{4,5},{5,4},{6,7},{7,6},{8,9},{9,8},{10,11... | collective-permute-start | bytes 1179656 | tf_op jit(solution)/shard_map/ppermute | solution.py:145
  721.5 12.6 %copy-start.2 = (f32[6,64,128]{2,1,0:T(8,128)S(1)}, f32[6,64,128]{2,1,0:T(8,128)}, u32[]{:S(2)}) copy-start(f32[6,64,128]{2,1,0:T(8,128)} %param.9) | copy-start | bytes 589828
Sparse Core Ops, SparseCore 0:
  12.2 432.7 all-gather.1

commit v8 on v7

--- a/solution.py
+++ b/solution.py
@@ -28,21 +28,23 @@
     return spread.astype(jnp.bfloat16).reshape(place_table.shape[2] * B, children * WJ)
 
 
-def block_product_kernel(src_ref, far_ref, pick_ref, flip_ref, pool_ref, swap_ref, rows_ref, out_ref, acc_ref):
-    t = pl.program_id(1)
-    at = pl.program_id(0) * pl.num_programs(1) + t
+def block_product_kernel(src_ref, far_ref, pick_ref, flip_ref, pool_ref, swap_ref, rows_ref, out_ref):
+    t = pl.program_id(0)
+    u = pl.program_id(1)
+    at = u * pl.num_programs(0) + t
+    width = pool_ref.shape[1]
+    block = jnp.where(pick_ref[at] == 0, pool_ref[0], swap_ref[0])
+    block = lax.cond(flip_ref[at] == 1, lambda b: b.T, lambda b: b, block)
+    contrib = jnp.dot(block, rows_ref[0], preferred_element_type=jnp.float32)
+    rows = pl.ds(pl.multiple_of(u * width, width), width)
 
     @pl.when(t == 0)
     def _():
-        acc_ref[...] = jnp.zeros_like(acc_ref)
+        out_ref[rows, :] = contrib
 
-    block = jnp.where(pick_ref[at] == 0, pool_ref[0], swap_ref[0])
-    block = lax.cond(flip_ref[at] == 1, lambda b: b.T, lambda b: b, block)
-    acc_ref[...] += jnp.dot(block, rows_ref[0], preferred_element_type=jnp.float32)
-
-    @pl.when(t == pl.num_programs(1) - 1)
+    @pl.when(t > 0)
     def _():
-        out_ref[...] = acc_ref[...]
+        out_ref[rows, :] += contrib
 
 
 def symmetric_product(ancestor_sigma, panel_rows, row_position, snode_position, snode_devices):
@@ -81,14 +83,13 @@
 
     grid_spec = pltpu.PrefetchScalarGridSpec(
         num_scalar_prefetch=4,
-        grid=(half, snode_devices),
+        grid=(snode_devices, half),
         in_specs=[
-            pl.BlockSpec((1, width, width), lambda i, j, s, f, p, q: (s[i * snode_devices + j], 0, 0)),
-            pl.BlockSpec((1, width, width), lambda i, j, s, f, p, q: (f[i * snode_devices + j], 0, 0)),
-            pl.BlockSpec((1, width, cols), lambda i, j, s, f, p, q: (j, 0, 0)),
+            pl.BlockSpec((1, width, width), lambda j, i, s, f, p, q: (s[i * snode_devices + j], 0, 0)),
+            pl.BlockSpec((1, width, width), lambda j, i, s, f, p, q: (f[i * snode_devices + j], 0, 0)),
+            pl.BlockSpec((1, width, cols), lambda j, i, s, f, p, q: (j, 0, 0)),
         ],
-        out_specs=pl.BlockSpec((width, cols), lambda i, j, s, f, p, q: (i, 0)),
-        scratch_shapes=[pltpu.VMEM((width, cols), jnp.float32)],
+        out_specs=pl.BlockSpec((half * width, cols), lambda j, i, s, f, p, q: (0, 0)),
     )
     return pl.pallas_call(
         block_product_kernel,
@@ -113,6 +114,7 @@
     place_bf = placed.astype(jnp.bfloat16)
     if row_devices == 2:
         partner = lax.ppermute(child_panels, "row", [(0, 1), (1, 0)])
+        ancestor_sigma, partner = lax.optimization_barrier((ancestor_sigma, partner))
         first = row_positions == 0
         gathered = jnp.concatenate(
             [jnp.where(first, child_panels, partner), jnp.where(first, partner, child_panels)], axis=1

time: 746 us -> 736 us (0.987)
  no operation moved by 1% of the time
where the time goes in v8:
time: 736 us; the launch traced here: 732 us
  waiting for transfers between devices  438 us (60%)
  Pallas kernels  144 us (20%)
  local copies, waits for them, and re-layouts  89.9 us (12%)
  matrix products  25.3 us (3%)
  other arithmetic  19.1 us (3%)
  between operations  14.2 us (2%)
    all_gather x1, waiting for transfers between devices, symmetric_product(): gathered = lax.all_gather(jnp.take(blocks, pick, axis=0), 'snode', axis=0)  433 us
    pallas_call x1, Pallas kernels, symmetric_product(): pl.pallas_call(block_product_kernel, grid_spec=grid_spec, out_shape=jax.S...  144 us
    another operation x2, local copies, waits for them, and re-layouts, symmetric_product(): panel_rows.reshape(snode_devices, width, cols)  40.2 us
  transfers between devices with their start and end apart: 4, of which 2 were waited for; matrix products, arithmetic and copies ran while one was open for 12% of the time, Pallas kernels for 0%

profile of v8, /device:TPU:0, one launch (start us, length us, event | category | flops | bytes accessed | tf_op | source)
XLA Modules:
  0.0 732.4 jit_solution(3220577852121516562)
XLA Ops:
  7.2 0.5 collective-permute-start
  7.8 5.5 collective-permute-done
  13.2 1.7 copy-done.2
  14.9 2.9 gather_fusion
  17.8 1.8 bitcast_select_fusion
  19.7 432.8 %all-gather.2.cloned.1.call-done = bf16[16,5,512,512]{3,2,1,0:T(8,128)(2,1)} async-done(((bf16[1,5,512,512]{3,2,1,0:T(8,128)(2,1)}), bf16[16,5,512,512]{3,2,1,0:T(8,128)(2,1)}) %all-gather.2.cloned.1.call-update) | async-done | bytes 41943056 | tf_op jit(solution)/shard_map/all_gather | solution.py:59
  452.5 13.7 %constant_dynamic-slice_fusion.1 = bf16[8,4,512,512]{3,2,1,0:T(8,128)(2,1)} fusion(bf16[16,5,512,512]{3,2,1,0:T(8,128)(2,1)} %all-gather.2.cloned.1.call-done, s32[]{:T(128)S(6)} %select_n.204), kind=kLoop, calls=%fused_computation.52 | loop fusion | bytes 33554436 | tf_op jit(solution)/shard_map/slice | solution.py:61
  467.0 0.3 select_reduce_fusion
  467.8 0.5 select_convert_fusion
  468.4 0.6 broadcast_select_fusion.2
  469.0 2.3 broadcast_select_fusion.1
  471.3 0.4 pad_maximum_fusion
  471.7 7.1 convert_bitcast_fusion
  478.8 13.7 %copy.47 = bf16[64,128,6,128]{3,2,1,0:T(8,128)(2,1)} copy(bf16[64,128,6,128]{3,0,1,2:T(8,128)(2,1)} %convert_bitcast_fusion) | data formatting | bytes 25165824 | tf_op jit(solution)/shard_map/reshape;reshape | solution.py:98
  492.6 26.5 %reshape.273.rows_ref = bf16[16,512,768]{2,1,0:T(8,128)(2,1)} reshape(bf16[64,128,6,128]{3,2,1,0:T(8,128)(2,1)} %copy.47) | data formatting | bytes 25165824 | tf_op jit(solution)/shard_map/reshape;reshape | solution.py:98
  519.0 7.1 convert_bitcast_fusion.1
  526.1 5.2 copy.37
  531.3 144.3 %shard_map.86 = f32[4096,768]{1,0:T(8,128)} custom-call(s32[128]{0:T(128)} %get-tuple-element.18.src_ref, s32[128]{0:T(128)} %get-tuple-element.17.far_ref, s32[128]{0:T(128)} %get-tuple-element.16.pick_ref, s32[128]{0:T(128)} %get-tuple-element.12.flip_ref, bf16[80,512,512]{2,1,0:T(8,128)(2,1)} %bitcast.37, bf16[32,512,512]{2,1,0:T(8,128)(2,1)} %bitcast.4.swap_ref, ...), custom_call_target="tpu_custom_call" | custom-call | tf_op jit(solution)/shard_map/pallas_call | solution.py:94
  675.7 12.6 %copy.36 = f32[4096,768]{0,1:T(8,128)} copy(f32[4096,768]{1,0:T(8,128)} %shard_map.86) | data formatting | bytes 25165824 | tf_op jit(solution)/shard_map/pallas_call | solution.py:94
  688.3 11.1 %fusion.22 = f32[6,128,128]{2,1,0:T(8,128)S(1)} fusion(bf16[4096,6,128]{2,0,1:T(8,128)(2,1)} %bitcast.40, f32[4096,6,128]{0,2,1:T(8,128)} %bitcast.35), kind=kOutput, calls=%fused_computation.73 | convolution fusion | flops 4831838208 | bytes 19267584 | tf_op jit(solution)/shard_map/nca,ncb->cab/dot_general | solution.py:142
  699.4 0.7 collective-permute-start.2
  700.1 12.0 %multiply_multiply_fusion = f32[4096,6,128]{0,2,1:T(8,128)} fusion(f32[4096,6,128]{0,2,1:T(8,128)} %bitcast.36, f32[6,128]{1,0:T(8,128)S(1)} %get-tuple-element.19, f32[4096,6]{0,1:T(8,128)S(1)} %bitcast.42), kind=kLoop, calls=%fused_computation.1 | loop fusion | flops 9437184 | bytes 25267200 | tf_op jit(solution)/shard_map/mul | solution.py:165
  712.1 12.6 %copy.40 = f32[4096,6,128]{2,0,1:T(8,128)} copy(f32[4096,6,128]{0,2,1:T(8,128)} %multiply_multiply_fusion) | data formatting | bytes 25165824
  724.7 0.8 fusion.5
  (48 shorter events, 1.4 us)
Async XLA Ops:
  7.2 445.3 %all-gather.2.cloned.1.call-start = ((), (), s32[]{:S(2)}) async-start(), calls=%async_computation | async-start | bytes 44564480 | tf_op jit(solution)/shard_map/all_gather | solution.py:59
  7.2 6.0 collective-permute-start
  13.2 1.7 copy-start.2
  19.7 447.3 %copy-start.4 = (s32[6,32]{1,0:T(8,128)S(1)}, s32[6,32]{1,0:T(8,128)}, u32[]{:S(2)}) copy-start(s32[6,32]{1,0:T(8,128)} %param.10) | copy-start | bytes 2308
  19.7 447.3 %copy-start.5 = (s32[64]{0:T(128)S(1)}, s32[64]{0:T(128)}, u32[]{:S(2)}) copy-start(s32[64]{0:T(128)} %param.13) | copy-start | bytes 772
  19.7 447.5 %copy-start.7 = (s32[6]{0:T(128)S(1)}, s32[6]{0:T(128)}, u32[]{:S(2)}) copy-start(s32[6]{0:T(128)} %param.11) | copy-start | bytes 76
  19.7 448.0 %copy-start.6 = (s32[6]{0:T(128)S(1)}, s32[6]{0:T(128)}, u32[]{:S(2)}) copy-start(s32[6]{0:T(128)} %param.12) | copy-start | bytes 76
  19.7 449.3 %copy-start.1 = (bf16[6,2048,128]{2,1,0:T(8,128)(2,1)S(1)}, bf16[6,2048,128]{2,1,0:T(8,128)(2,1)}, u32[]{:S(2)}) copy-start(bf16[6,2048,128]{2,1,0:T(8,128)(2,1)} %param.8) | copy-start | bytes 9437188
  466.2 65.1 %collective-permute-start.1 = (bf16[8,4,512,512]{3,2,1,0:T(8,128)(2,1)}, bf16[8,4,512,512]{3,2,1,0:T(8,128)(2,1)}, u32[]{:S(2)}, u32[]{:S(2)}) collective-permute-start(bf16[8,4,512,512]{3,2,1,0:T(8,128)(2,1)} %constant_dynamic-slice_fusion.1), channel_id=1, source_target_pairs={{0,1},{1,0},{2,3},{3,2},{4,5},{5,4},{6,7},{7,6},{8,9},{9,8},{10,11... | collective-permute-start | bytes 50331656 | tf_op jit(solution)/shard_map/ppermute | solution.py:61
  471.7 7.1 copy-start
  699.4 25.3 %collective-permute-start.2 = (f32[6,128,128]{2,1,0:T(8,128)S(1)}, f32[6,128,128]{2,1,0:T(8,128)S(1)}, u32[]{:S(2)}, u32[]{:S(2)}) collective-permute-start(f32[6,128,128]{2,1,0:T(8,128)S(1)} %fusion.22), channel_id=1, source_target_pairs={{0,1},{1,0},{2,3},{3,2},{4,5},{5,4},{6,7},{7,6},{8,9},{9,8},{10,11... | collective-permute-start | bytes 1179656 | tf_op jit(solution)/shard_map/ppermute | solution.py:147
  712.1 12.6 %copy-start.3 = (f32[6,64,128]{2,1,0:T(8,128)S(1)}, f32[6,64,128]{2,1,0:T(8,128)}, u32[]{:S(2)}) copy-start(f32[6,64,128]{2,1,0:T(8,128)} %param.9) | copy-start | bytes 589828
Sparse Core Ops, SparseCore 0:
  19.8 432.6 all-gather.1

commit v9 on v8

--- a/solution.py
+++ b/solution.py
@@ -114,7 +114,6 @@
     place_bf = placed.astype(jnp.bfloat16)
     if row_devices == 2:
         partner = lax.ppermute(child_panels, "row", [(0, 1), (1, 0)])
-        ancestor_sigma, partner = lax.optimization_barrier((ancestor_sigma, partner))
         first = row_positions == 0
         gathered = jnp.concatenate(
             [jnp.where(first, child_panels, partner), jnp.where(first, partner, child_panels)], axis=1

time: 736 us -> 740 us (level)
  no operation moved by 1% of the time
where the time goes in v9:
time: 740 us; the launch traced here: 737 us
  waiting for transfers between devices  445 us (60%)
  Pallas kernels  144 us (19%)
  local copies, waits for them, and re-layouts  88.2 us (12%)
  matrix products  25.3 us (3%)
  other arithmetic  19.1 us (3%)
  between operations  14.3 us (2%)
    all_gather x1, waiting for transfers between devices, symmetric_product(): gathered = lax.all_gather(jnp.take(blocks, pick, axis=0), 'snode', axis=0)  433 us
    pallas_call x1, Pallas kernels, symmetric_product(): pl.pallas_call(block_product_kernel, grid_spec=grid_spec, out_shape=jax.S...  144 us
    another operation x2, local copies, waits for them, and re-layouts, symmetric_product(): panel_rows.reshape(snode_devices, width, cols)  40.2 us
  transfers between devices with their start and end apart: 4, of which 2 were waited for; matrix products, arithmetic and copies ran while one was open for 12% of the time, Pallas kernels for 0%

profile of v9, /device:TPU:0, one launch (start us, length us, event | category | flops | bytes accessed | tf_op | source)
XLA Modules:
  0.0 736.9 jit_solution(17623594660941700557)
XLA Ops:
  7.3 2.9 gather_fusion
  10.2 1.8 bitcast_select_fusion
  12.1 432.8 %all-gather.2.cloned.1.call-done = bf16[16,5,512,512]{3,2,1,0:T(8,128)(2,1)} async-done(((bf16[1,5,512,512]{3,2,1,0:T(8,128)(2,1)}), bf16[16,5,512,512]{3,2,1,0:T(8,128)(2,1)}) %all-gather.2.cloned.1.call-update) | async-done | bytes 41943056 | tf_op jit(solution)/shard_map/all_gather | solution.py:59
  444.9 13.7 %constant_dynamic-slice_fusion.1 = bf16[8,4,512,512]{3,2,1,0:T(8,128)(2,1)} fusion(bf16[16,5,512,512]{3,2,1,0:T(8,128)(2,1)} %all-gather.2.cloned.1.call-done, s32[]{:T(128)S(6)} %select_n.204), kind=kLoop, calls=%fused_computation.52 | loop fusion | bytes 33554436 | tf_op jit(solution)/shard_map/slice | solution.py:61
  458.7 0.5 collective-permute-start.1
  459.9 0.3 select_reduce_fusion
  460.2 0.1 convert_reduce_fusion
  460.8 0.5 select_convert_fusion
  461.3 0.6 broadcast_select_fusion.2
  461.9 11.7 %collective-permute-done.1 = bf16[6,2048,128]{2,1,0:T(8,128)(2,1)} collective-permute-done((bf16[6,2048,128]{2,1,0:T(8,128)(2,1)S(1)}, bf16[6,2048,128]{2,1,0:T(8,128)(2,1)}, u32[]{:S(2)}, u32[]{:S(2)}) %collective-permute-start.1) | collective-permute-done | bytes 3145760 | tf_op jit(solution)/shard_map/ppermute | solution.py:116
  473.7 2.3 broadcast_select_fusion.1
  476.0 0.4 pad_maximum_fusion
  476.4 7.1 convert_bitcast_fusion
  483.5 13.7 %copy.47 = bf16[64,128,6,128]{3,2,1,0:T(8,128)(2,1)} copy(bf16[64,128,6,128]{3,0,1,2:T(8,128)(2,1)} %convert_bitcast_fusion) | data formatting | bytes 25165824 | tf_op jit(solution)/shard_map/reshape;reshape | solution.py:98
  497.2 26.5 %reshape.273.rows_ref = bf16[16,512,768]{2,1,0:T(8,128)(2,1)} reshape(bf16[64,128,6,128]{3,2,1,0:T(8,128)(2,1)} %copy.47) | data formatting | bytes 25165824 | tf_op jit(solution)/shard_map/reshape;reshape | solution.py:98
  523.7 7.1 convert_bitcast_fusion.1
  530.8 5.2 copy.37
  536.0 144.3 %shard_map.86 = f32[4096,768]{1,0:T(8,128)} custom-call(s32[128]{0:T(128)} %get-tuple-element.14.src_ref, s32[128]{0:T(128)} %get-tuple-element.13.far_ref, s32[128]{0:T(128)} %get-tuple-element.12.pick_ref, s32[128]{0:T(128)} %get-tuple-element.8.flip_ref, bf16[80,512,512]{2,1,0:T(8,128)(2,1)} %bitcast.37, bf16[32,512,512]{2,1,0:T(8,128)(2,1)} %bitcast.4.swap_ref, ...), custom_call_target="tpu_custom_call" | custom-call | tf_op jit(solution)/shard_map/pallas_call | solution.py:94
  680.4 12.6 %copy.36 = f32[4096,768]{0,1:T(8,128)} copy(f32[4096,768]{1,0:T(8,128)} %shard_map.86) | data formatting | bytes 25165824 | tf_op jit(solution)/shard_map/pallas_call | solution.py:94
  693.0 11.1 %fusion.22 = f32[6,128,128]{2,1,0:T(8,128)S(1)} fusion(bf16[4096,6,128]{2,0,1:T(8,128)(2,1)} %bitcast.40, f32[4096,6,128]{0,2,1:T(8,128)} %bitcast.35), kind=kOutput, calls=%fused_computation.73 | convolution fusion | flops 4831838208 | bytes 19267584 | tf_op jit(solution)/shard_map/nca,ncb->cab/dot_general | solution.py:141
  704.1 0.6 collective-permute-start.2
  704.6 12.0 %multiply_multiply_fusion = f32[4096,6,128]{0,2,1:T(8,128)} fusion(f32[4096,6,128]{0,2,1:T(8,128)} %bitcast.36, f32[6,128]{1,0:T(8,128)S(1)} %get-tuple-element.15, f32[4096,6]{0,1:T(8,128)S(1)} %bitcast.42), kind=kLoop, calls=%fused_computation.1 | loop fusion | flops 9437184 | bytes 25267200 | tf_op jit(solution)/shard_map/mul | solution.py:164
  716.6 12.6 %copy.40 = f32[4096,6,128]{2,0,1:T(8,128)} copy(f32[4096,6,128]{0,2,1:T(8,128)} %multiply_multiply_fusion) | data formatting | bytes 25165824
  729.3 0.8 fusion.5
  (46 shorter events, 1.3 us)
Async XLA Ops:
  7.2 437.8 %all-gather.2.cloned.1.call-start = ((), (), s32[]{:S(2)}) async-start(), calls=%async_computation | async-start | bytes 44564480 | tf_op jit(solution)/shard_map/all_gather | solution.py:59
  12.0 446.6 %copy-start.1 = (bf16[6,2048,128]{2,1,0:T(8,128)(2,1)S(1)}, bf16[6,2048,128]{2,1,0:T(8,128)(2,1)}, u32[]{:S(2)}) copy-start(bf16[6,2048,128]{2,1,0:T(8,128)(2,1)} %param.8) | copy-start | bytes 9437188
  12.0 447.8 %copy-start.3 = (s32[6,32]{1,0:T(8,128)S(1)}, s32[6,32]{1,0:T(8,128)}, u32[]{:S(2)}) copy-start(s32[6,32]{1,0:T(8,128)} %param.10) | copy-start | bytes 2308
  12.1 447.8 %copy-start.4 = (s32[64]{0:T(128)S(1)}, s32[64]{0:T(128)}, u32[]{:S(2)}) copy-start(s32[64]{0:T(128)} %param.13) | copy-start | bytes 772
  12.1 448.1 %copy-start.6 = (s32[6]{0:T(128)S(1)}, s32[6]{0:T(128)}, u32[]{:S(2)}) copy-start(s32[6]{0:T(128)} %param.11) | copy-start | bytes 76
  12.1 448.5 %copy-start.5 = (s32[6]{0:T(128)S(1)}, s32[6]{0:T(128)}, u32[]{:S(2)}) copy-start(s32[6]{0:T(128)} %param.12) | copy-start | bytes 76
  458.7 77.4 %collective-permute-start = (bf16[8,4,512,512]{3,2,1,0:T(8,128)(2,1)}, bf16[8,4,512,512]{3,2,1,0:T(8,128)(2,1)}, u32[]{:S(2)}, u32[]{:S(2)}) collective-permute-start(bf16[8,4,512,512]{3,2,1,0:T(8,128)(2,1)} %constant_dynamic-slice_fusion.1), channel_id=1, source_target_pairs={{0,1},{1,0},{2,3},{3,2},{4,5},{5,4},{6,7},{7,6},{8,9},{9,8},{10,11... | collective-permute-start | bytes 50331656 | tf_op jit(solution)/shard_map/ppermute | solution.py:61
  458.7 15.0 %collective-permute-start.1 = (bf16[6,2048,128]{2,1,0:T(8,128)(2,1)S(1)}, bf16[6,2048,128]{2,1,0:T(8,128)(2,1)}, u32[]{:S(2)}, u32[]{:S(2)}) collective-permute-start(bf16[6,2048,128]{2,1,0:T(8,128)(2,1)S(1)} %copy-done.1), channel_id=1, source_target_pairs={{0,1},{1,0},{2,3},{3,2},{4,5},{5,4},{6,7},{7,6},{8,9},{9,8},{10,11... | collective-permute-start | bytes 9437192 | tf_op jit(solution)/shard_map/ppermute | solution.py:116
  476.4 7.1 copy-start
  704.1 25.2 %collective-permute-start.2 = (f32[6,128,128]{2,1,0:T(8,128)S(1)}, f32[6,128,128]{2,1,0:T(8,128)S(1)}, u32[]{:S(2)}, u32[]{:S(2)}) collective-permute-start(f32[6,128,128]{2,1,0:T(8,128)S(1)} %fusion.22), channel_id=1, source_target_pairs={{0,1},{1,0},{2,3},{3,2},{4,5},{5,4},{6,7},{7,6},{8,9},{9,8},{10,11... | collective-permute-start | bytes 1179656 | tf_op jit(solution)/shard_map/ppermute | solution.py:146
  716.6 12.6 %copy-start.2 = (f32[6,64,128]{2,1,0:T(8,128)S(1)}, f32[6,64,128]{2,1,0:T(8,128)}, u32[]{:S(2)}) copy-start(f32[6,64,128]{2,1,0:T(8,128)} %param.9) | copy-start | bytes 589828
Sparse Core Ops, SparseCore 0:
  12.2 432.7 all-gather.1

commit v10 on v8

--- a/solution.py
+++ b/solution.py
@@ -33,9 +33,18 @@
     u = pl.program_id(1)
     at = u * pl.num_programs(0) + t
     width = pool_ref.shape[1]
-    block = jnp.where(pick_ref[at] == 0, pool_ref[0], swap_ref[0])
-    block = lax.cond(flip_ref[at] == 1, lambda b: b.T, lambda b: b, block)
-    contrib = jnp.dot(block, rows_ref[0], preferred_element_type=jnp.float32)
+    def product_of(block):
+        return jnp.dot(block, rows_ref[0], preferred_element_type=jnp.float32)
+
+    contrib = lax.cond(
+        pick_ref[at] == 0,
+        lambda: lax.cond(
+            flip_ref[at] == 1,
+            lambda: product_of(pool_ref[0].T),
+            lambda: product_of(pool_ref[0]),
+        ),
+        lambda: product_of(swap_ref[0].T),
+    )
     rows = pl.ds(pl.multiple_of(u * width, width), width)
 
     @pl.when(t == 0)

time: 736 us -> 793 us (1.077)
  Pallas kernels: 144 us -> 203 us
    pallas_call x1, Pallas kernels: 144 us -> 203 us  [symmetric_product(): pl.pallas_call(block_product_kernel, grid_spec=grid_spec, out_shape=jax.S...]
  transfers between devices with their start and end apart: 4 -> 4, of which waited for: 2 -> 2; matrix products, arithmetic and copies ran while one was open for 12% -> 11% of each run, Pallas kernels for 0% -> 0%
where the time goes in v10:
time: 793 us; the launch traced here: 791 us
  waiting for transfers between devices  438 us (55%)
  Pallas kernels  203 us (26%)
  local copies, waits for them, and re-layouts  89.9 us (11%)
  matrix products  25.3 us (3%)
  other arithmetic  19.1 us (2%)
  between operations  14.2 us (2%)
    all_gather x1, waiting for transfers between devices, symmetric_product(): gathered = lax.all_gather(jnp.take(blocks, pick, axis=0), 'snode', axis=0)  433 us
    pallas_call x1, Pallas kernels, symmetric_product(): pl.pallas_call(block_product_kernel, grid_spec=grid_spec, out_shape=jax.S...  203 us
    another operation x2, local copies, waits for them, and re-layouts, symmetric_product(): panel_rows.reshape(snode_devices, width, cols)  40.2 us
  transfers between devices with their start and end apart: 4, of which 2 were waited for; matrix products, arithmetic and copies ran while one was open for 11% of the time, Pallas kernels for 0%

profile of v10, /device:TPU:0, one launch (start us, length us, event | category | flops | bytes accessed | tf_op | source)
XLA Modules:
  0.0 791.5 jit_solution(17378973022054779120)
XLA Ops:
  7.2 0.5 collective-permute-start
  7.8 5.5 collective-permute-done
  13.2 1.7 copy-done.2
  14.9 2.9 gather_fusion
  17.8 1.8 bitcast_select_fusion
  19.7 432.8 %all-gather.2.cloned.1.call-done = bf16[16,5,512,512]{3,2,1,0:T(8,128)(2,1)} async-done(((bf16[1,5,512,512]{3,2,1,0:T(8,128)(2,1)}), bf16[16,5,512,512]{3,2,1,0:T(8,128)(2,1)}) %all-gather.2.cloned.1.call-update) | async-done | bytes 41943056 | tf_op jit(solution)/shard_map/all_gather | solution.py:68
  452.5 13.7 %constant_dynamic-slice_fusion.1 = bf16[8,4,512,512]{3,2,1,0:T(8,128)(2,1)} fusion(bf16[16,5,512,512]{3,2,1,0:T(8,128)(2,1)} %all-gather.2.cloned.1.call-done, s32[]{:T(128)S(6)} %select_n.204), kind=kLoop, calls=%fused_computation.52 | loop fusion | bytes 33554436 | tf_op jit(solution)/shard_map/slice | solution.py:70
  467.0 0.3 select_reduce_fusion
  467.8 0.5 select_convert_fusion
  468.4 0.6 broadcast_select_fusion.2
  469.0 2.3 broadcast_select_fusion.1
  471.3 0.4 pad_maximum_fusion
  471.7 7.1 convert_bitcast_fusion
  478.8 13.7 %copy.47 = bf16[64,128,6,128]{3,2,1,0:T(8,128)(2,1)} copy(bf16[64,128,6,128]{3,0,1,2:T(8,128)(2,1)} %convert_bitcast_fusion) | data formatting | bytes 25165824 | tf_op jit(solution)/shard_map/reshape;reshape | solution.py:107
  492.6 26.5 %reshape.273.rows_ref = bf16[16,512,768]{2,1,0:T(8,128)(2,1)} reshape(bf16[64,128,6,128]{3,2,1,0:T(8,128)(2,1)} %copy.47) | data formatting | bytes 25165824 | tf_op jit(solution)/shard_map/reshape;reshape | solution.py:107
  519.0 7.1 convert_bitcast_fusion.1
  526.1 5.2 copy.37
  531.3 203.4 %shard_map.86 = f32[4096,768]{1,0:T(8,128)} custom-call(s32[128]{0:T(128)} %get-tuple-element.18.src_ref, s32[128]{0:T(128)} %get-tuple-element.17.far_ref, s32[128]{0:T(128)} %get-tuple-element.16.pick_ref, s32[128]{0:T(128)} %get-tuple-element.12.flip_ref, bf16[80,512,512]{2,1,0:T(8,128)(2,1)} %bitcast.37, bf16[32,512,512]{2,1,0:T(8,128)(2,1)} %bitcast.4.swap_ref, ...), custom_call_target="tpu_custom_call" | custom-call | tf_op jit(solution)/shard_map/pallas_call | solution.py:103
  734.7 12.6 %copy.36 = f32[4096,768]{0,1:T(8,128)} copy(f32[4096,768]{1,0:T(8,128)} %shard_map.86) | data formatting | bytes 25165824 | tf_op jit(solution)/shard_map/pallas_call | solution.py:103
  747.3 11.1 %fusion.22 = f32[6,128,128]{2,1,0:T(8,128)S(1)} fusion(bf16[4096,6,128]{2,0,1:T(8,128)(2,1)} %bitcast.40, f32[4096,6,128]{0,2,1:T(8,128)} %bitcast.35), kind=kOutput, calls=%fused_computation.73 | convolution fusion | flops 4831838208 | bytes 19267584 | tf_op jit(solution)/shard_map/nca,ncb->cab/dot_general | solution.py:151
  758.4 0.8 collective-permute-start.2
  759.2 12.0 %multiply_multiply_fusion = f32[4096,6,128]{0,2,1:T(8,128)} fusion(f32[4096,6,128]{0,2,1:T(8,128)} %bitcast.36, f32[6,128]{1,0:T(8,128)S(1)} %get-tuple-element.19, f32[4096,6]{0,1:T(8,128)S(1)} %bitcast.42), kind=kLoop, calls=%fused_computation.1 | loop fusion | flops 9437184 | bytes 25267200 | tf_op jit(solution)/shard_map/mul | solution.py:174
  771.2 12.6 %copy.40 = f32[4096,6,128]{2,0,1:T(8,128)} copy(f32[4096,6,128]{0,2,1:T(8,128)} %multiply_multiply_fusion) | data formatting | bytes 25165824
  783.8 0.8 fusion.5
  (48 shorter events, 1.4 us)
Async XLA Ops:
  7.2 445.3 %all-gather.2.cloned.1.call-start = ((), (), s32[]{:S(2)}) async-start(), calls=%async_computation | async-start | bytes 44564480 | tf_op jit(solution)/shard_map/all_gather | solution.py:68
  7.2 6.0 collective-permute-start
  13.2 1.7 copy-start.2
  19.7 447.3 %copy-start.4 = (s32[6,32]{1,0:T(8,128)S(1)}, s32[6,32]{1,0:T(8,128)}, u32[]{:S(2)}) copy-start(s32[6,32]{1,0:T(8,128)} %param.10) | copy-start | bytes 2308
  19.7 447.3 %copy-start.5 = (s32[64]{0:T(128)S(1)}, s32[64]{0:T(128)}, u32[]{:S(2)}) copy-start(s32[64]{0:T(128)} %param.13) | copy-start | bytes 772
  19.7 447.5 %copy-start.7 = (s32[6]{0:T(128)S(1)}, s32[6]{0:T(128)}, u32[]{:S(2)}) copy-start(s32[6]{0:T(128)} %param.11) | copy-start | bytes 76
  19.7 448.0 %copy-start.6 = (s32[6]{0:T(128)S(1)}, s32[6]{0:T(128)}, u32[]{:S(2)}) copy-start(s32[6]{0:T(128)} %param.12) | copy-start | bytes 76
  19.7 449.3 %copy-start.1 = (bf16[6,2048,128]{2,1,0:T(8,128)(2,1)S(1)}, bf16[6,2048,128]{2,1,0:T(8,128)(2,1)}, u32[]{:S(2)}) copy-start(bf16[6,2048,128]{2,1,0:T(8,128)(2,1)} %param.8) | copy-start | bytes 9437188
  466.2 65.1 %collective-permute-start.1 = (bf16[8,4,512,512]{3,2,1,0:T(8,128)(2,1)}, bf16[8,4,512,512]{3,2,1,0:T(8,128)(2,1)}, u32[]{:S(2)}, u32[]{:S(2)}) collective-permute-start(bf16[8,4,512,512]{3,2,1,0:T(8,128)(2,1)} %constant_dynamic-slice_fusion.1), channel_id=1, source_target_pairs={{0,1},{1,0},{2,3},{3,2},{4,5},{5,4},{6,7},{7,6},{8,9},{9,8},{10,11... | collective-permute-start | bytes 50331656 | tf_op jit(solution)/shard_map/ppermute | solution.py:70
  471.7 7.1 copy-start
  758.4 25.4 %collective-permute-start.2 = (f32[6,128,128]{2,1,0:T(8,128)S(1)}, f32[6,128,128]{2,1,0:T(8,128)S(1)}, u32[]{:S(2)}, u32[]{:S(2)}) collective-permute-start(f32[6,128,128]{2,1,0:T(8,128)S(1)} %fusion.22), channel_id=1, source_target_pairs={{0,1},{1,0},{2,3},{3,2},{4,5},{5,4},{6,7},{7,6},{8,9},{9,8},{10,11... | collective-permute-start | bytes 1179656 | tf_op jit(solution)/shard_map/ppermute | solution.py:156
  771.2 12.6 %copy-start.3 = (f32[6,64,128]{2,1,0:T(8,128)S(1)}, f32[6,64,128]{2,1,0:T(8,128)}, u32[]{:S(2)}) copy-start(f32[6,64,128]{2,1,0:T(8,128)} %param.9) | copy-start | bytes 589828
Sparse Core Ops, SparseCore 0:
  19.8 432.6 all-gather.1

commit v11 on v8

--- a/solution.py
+++ b/solution.py
@@ -34,7 +34,7 @@
     at = u * pl.num_programs(0) + t
     width = pool_ref.shape[1]
     block = jnp.where(pick_ref[at] == 0, pool_ref[0], swap_ref[0])
-    block = lax.cond(flip_ref[at] == 1, lambda b: b.T, lambda b: b, block)
+    block = jnp.where(flip_ref[at] == 1, block.T, block)
     contrib = jnp.dot(block, rows_ref[0], preferred_element_type=jnp.float32)
     rows = pl.ds(pl.multiple_of(u * width, width), width)
 

time: 736 us -> 723 us (0.982)
  Pallas kernels: 144 us -> 131 us
    pallas_call x1, Pallas kernels: 144 us -> 131 us  [symmetric_product(): pl.pallas_call(block_product_kernel, grid_spec=grid_spec, out_shape=jax.S...]
where the time goes in v11:
time: 723 us; the launch traced here: 719 us
  waiting for transfers between devices  438 us (61%)
  Pallas kernels  131 us (18%)
  local copies, waits for them, and re-layouts  89.9 us (12%)
  matrix products  25.3 us (3%)
  other arithmetic  19.1 us (3%)
  between operations  14.2 us (2%)
    all_gather x1, waiting for transfers between devices, symmetric_product(): gathered = lax.all_gather(jnp.take(blocks, pick, axis=0), 'snode', axis=0)  433 us
    pallas_call x1, Pallas kernels, symmetric_product(): pl.pallas_call(block_product_kernel, grid_spec=grid_spec, out_shape=jax.S...  131 us
    another operation x2, local copies, waits for them, and re-layouts, symmetric_product(): panel_rows.reshape(snode_devices, width, cols)  40.2 us
    unnamed x19, local copies, waits for them, and re-layouts  14.5 us
  transfers between devices with their start and end apart: 4, of which 2 were waited for; matrix products, arithmetic and copies ran while one was open for 12% of the time, Pallas kernels for 0%

profile of v11, /device:TPU:0, one launch (start us, length us, event | category | flops | bytes accessed | tf_op | source)
XLA Modules:
  0.0 719.0 jit_solution(11687814087160553604)
XLA Ops:
  7.2 0.5 collective-permute-start
  7.8 5.5 collective-permute-done
  13.2 1.7 copy-done.2
  14.9 2.9 gather_fusion
  17.8 1.8 bitcast_select_fusion
  19.7 432.8 %all-gather.2.cloned.1.call-done = bf16[16,5,512,512]{3,2,1,0:T(8,128)(2,1)} async-done(((bf16[1,5,512,512]{3,2,1,0:T(8,128)(2,1)}), bf16[16,5,512,512]{3,2,1,0:T(8,128)(2,1)}) %all-gather.2.cloned.1.call-update) | async-done | bytes 41943056 | tf_op jit(solution)/shard_map/all_gather | solution.py:59
  452.5 13.7 %constant_dynamic-slice_fusion.1 = bf16[8,4,512,512]{3,2,1,0:T(8,128)(2,1)} fusion(bf16[16,5,512,512]{3,2,1,0:T(8,128)(2,1)} %all-gather.2.cloned.1.call-done, s32[]{:T(128)S(6)} %select_n.204), kind=kLoop, calls=%fused_computation.52 | loop fusion | bytes 33554436 | tf_op jit(solution)/shard_map/slice | solution.py:61
  467.0 0.3 select_reduce_fusion
  467.8 0.5 select_convert_fusion
  468.4 0.6 broadcast_select_fusion.2
  469.0 2.3 broadcast_select_fusion.1
  471.3 0.4 pad_maximum_fusion
  471.7 7.1 convert_bitcast_fusion
  478.8 13.7 %copy.47 = bf16[64,128,6,128]{3,2,1,0:T(8,128)(2,1)} copy(bf16[64,128,6,128]{3,0,1,2:T(8,128)(2,1)} %convert_bitcast_fusion) | data formatting | bytes 25165824 | tf_op jit(solution)/shard_map/reshape;reshape | solution.py:98
  492.6 26.5 %reshape.273.rows_ref = bf16[16,512,768]{2,1,0:T(8,128)(2,1)} reshape(bf16[64,128,6,128]{3,2,1,0:T(8,128)(2,1)} %copy.47) | data formatting | bytes 25165824 | tf_op jit(solution)/shard_map/reshape;reshape | solution.py:98
  519.0 7.1 convert_bitcast_fusion.1
  526.1 5.2 copy.37
  531.3 131.1 %shard_map.86 = f32[4096,768]{1,0:T(8,128)} custom-call(s32[128]{0:T(128)} %get-tuple-element.18.src_ref, s32[128]{0:T(128)} %get-tuple-element.17.far_ref, s32[128]{0:T(128)} %get-tuple-element.16.pick_ref, s32[128]{0:T(128)} %get-tuple-element.12.flip_ref, bf16[80,512,512]{2,1,0:T(8,128)(2,1)} %bitcast.37, bf16[32,512,512]{2,1,0:T(8,128)(2,1)} %bitcast.4.swap_ref, ...), custom_call_target="tpu_custom_call" | custom-call | tf_op jit(solution)/shard_map/pallas_call | solution.py:94
  662.5 12.6 %copy.36 = f32[4096,768]{0,1:T(8,128)} copy(f32[4096,768]{1,0:T(8,128)} %shard_map.86) | data formatting | bytes 25165824 | tf_op jit(solution)/shard_map/pallas_call | solution.py:94
  675.1 11.1 %fusion.22 = f32[6,128,128]{2,1,0:T(8,128)S(1)} fusion(bf16[4096,6,128]{2,0,1:T(8,128)(2,1)} %bitcast.40, f32[4096,6,128]{0,2,1:T(8,128)} %bitcast.35), kind=kOutput, calls=%fused_computation.73 | convolution fusion | flops 4831838208 | bytes 19267584 | tf_op jit(solution)/shard_map/nca,ncb->cab/dot_general | solution.py:142
  686.2 0.5 collective-permute-start.2
  686.7 12.0 %multiply_multiply_fusion = f32[4096,6,128]{0,2,1:T(8,128)} fusion(f32[4096,6,128]{0,2,1:T(8,128)} %bitcast.36, f32[6,128]{1,0:T(8,128)S(1)} %get-tuple-element.19, f32[4096,6]{0,1:T(8,128)S(1)} %bitcast.42), kind=kLoop, calls=%fused_computation.1 | loop fusion | flops 9437184 | bytes 25267200 | tf_op jit(solution)/shard_map/mul | solution.py:165
  698.7 12.6 %copy.40 = f32[4096,6,128]{2,0,1:T(8,128)} copy(f32[4096,6,128]{0,2,1:T(8,128)} %multiply_multiply_fusion) | data formatting | bytes 25165824
  711.4 0.8 fusion.5
  (48 shorter events, 1.4 us)
Async XLA Ops:
  7.2 445.3 %all-gather.2.cloned.1.call-start = ((), (), s32[]{:S(2)}) async-start(), calls=%async_computation | async-start | bytes 44564480 | tf_op jit(solution)/shard_map/all_gather | solution.py:59
  7.2 6.0 collective-permute-start
  13.2 1.7 copy-start.2
  19.7 447.3 %copy-start.4 = (s32[6,32]{1,0:T(8,128)S(1)}, s32[6,32]{1,0:T(8,128)}, u32[]{:S(2)}) copy-start(s32[6,32]{1,0:T(8,128)} %param.10) | copy-start | bytes 2308
  19.7 447.3 %copy-start.5 = (s32[64]{0:T(128)S(1)}, s32[64]{0:T(128)}, u32[]{:S(2)}) copy-start(s32[64]{0:T(128)} %param.13) | copy-start | bytes 772
  19.7 447.5 %copy-start.7 = (s32[6]{0:T(128)S(1)}, s32[6]{0:T(128)}, u32[]{:S(2)}) copy-start(s32[6]{0:T(128)} %param.11) | copy-start | bytes 76
  19.7 448.0 %copy-start.6 = (s32[6]{0:T(128)S(1)}, s32[6]{0:T(128)}, u32[]{:S(2)}) copy-start(s32[6]{0:T(128)} %param.12) | copy-start | bytes 76
  19.7 449.3 %copy-start.1 = (bf16[6,2048,128]{2,1,0:T(8,128)(2,1)S(1)}, bf16[6,2048,128]{2,1,0:T(8,128)(2,1)}, u32[]{:S(2)}) copy-start(bf16[6,2048,128]{2,1,0:T(8,128)(2,1)} %param.8) | copy-start | bytes 9437188
  466.2 65.1 %collective-permute-start.1 = (bf16[8,4,512,512]{3,2,1,0:T(8,128)(2,1)}, bf16[8,4,512,512]{3,2,1,0:T(8,128)(2,1)}, u32[]{:S(2)}, u32[]{:S(2)}) collective-permute-start(bf16[8,4,512,512]{3,2,1,0:T(8,128)(2,1)} %constant_dynamic-slice_fusion.1), channel_id=1, source_target_pairs={{0,1},{1,0},{2,3},{3,2},{4,5},{5,4},{6,7},{7,6},{8,9},{9,8},{10,11... | collective-permute-start | bytes 50331656 | tf_op jit(solution)/shard_map/ppermute | solution.py:61
  471.7 7.1 copy-start
  686.2 25.2 %collective-permute-start.2 = (f32[6,128,128]{2,1,0:T(8,128)S(1)}, f32[6,128,128]{2,1,0:T(8,128)S(1)}, u32[]{:S(2)}, u32[]{:S(2)}) collective-permute-start(f32[6,128,128]{2,1,0:T(8,128)S(1)} %fusion.22), channel_id=1, source_target_pairs={{0,1},{1,0},{2,3},{3,2},{4,5},{5,4},{6,7},{7,6},{8,9},{9,8},{10,11... | collective-permute-start | bytes 1179656 | tf_op jit(solution)/shard_map/ppermute | solution.py:147
  698.7 12.6 %copy-start.3 = (f32[6,64,128]{2,1,0:T(8,128)S(1)}, f32[6,64,128]{2,1,0:T(8,128)}, u32[]{:S(2)}) copy-start(f32[6,64,128]{2,1,0:T(8,128)} %param.9) | copy-start | bytes 589828
Sparse Core Ops, SparseCore 0:
  19.8 432.6 all-gather.1

commit v12 on v11

--- a/solution.py
+++ b/solution.py
@@ -35,7 +35,7 @@
     width = pool_ref.shape[1]
     block = jnp.where(pick_ref[at] == 0, pool_ref[0], swap_ref[0])
     block = jnp.where(flip_ref[at] == 1, block.T, block)
-    contrib = jnp.dot(block, rows_ref[0], preferred_element_type=jnp.float32)
+    contrib = jnp.dot(block, rows_ref[...], preferred_element_type=jnp.float32)
     rows = pl.ds(pl.multiple_of(u * width, width), width)
 
     @pl.when(t == 0)
@@ -87,7 +87,7 @@
         in_specs=[
             pl.BlockSpec((1, width, width), lambda j, i, s, f, p, q: (s[i * snode_devices + j], 0, 0)),
             pl.BlockSpec((1, width, width), lambda j, i, s, f, p, q: (f[i * snode_devices + j], 0, 0)),
-            pl.BlockSpec((1, width, cols), lambda j, i, s, f, p, q: (j, 0, 0)),
+            pl.BlockSpec((width, cols), lambda j, i, s, f, p, q: (j, 0)),
         ],
         out_specs=pl.BlockSpec((half * width, cols), lambda j, i, s, f, p, q: (0, 0)),
     )
@@ -95,7 +95,7 @@
         block_product_kernel,
         grid_spec=grid_spec,
         out_shape=jax.ShapeDtypeStruct((half * width, cols), jnp.float32),
-    )(*tables, pool, swap, panel_rows.reshape(snode_devices, width, cols))
+    )(*tables, pool, swap, panel_rows)
 
 def body(
     ancestor_sigma,

time: 723 us -> 703 us (0.972)
  local copies, waits for them, and re-layouts: 89.9 us -> 74.2 us
    another operation x2 -> x0, local copies, waits for them, and re-layouts: 40.2 us -> none  [symmetric_product(): panel_rows.reshape(snode_devices, width, cols)]
    reshape x0 -> x1, local copies, waits for them, and re-layouts: none -> 12.4 us  [expand_rows(): spread.astype(jnp.bfloat16).reshape(place_table.shape[2] * B, children * WJ)]
    unnamed x19 -> x18, local copies, waits for them, and re-layouts: 14.5 us -> 26.6 us
  transfers between devices with their start and end apart: 4 -> 4, of which waited for: 2 -> 2; matrix products, arithmetic and copies ran while one was open for 12% -> 10% of each run, Pallas kernels for 0% -> 0%
where the time goes in v12:
time: 703 us; the launch traced here: 700 us
  waiting for transfers between devices  438 us (62%)
  Pallas kernels  131 us (19%)
  local copies, waits for them, and re-layouts  74.2 us (11%)
  matrix products  22.1 us (3%)
  other arithmetic  19.1 us (3%)
  between operations  14.2 us (2%)
    all_gather x1, waiting for transfers between devices, symmetric_product(): gathered = lax.all_gather(jnp.take(blocks, pick, axis=0), 'snode', axis=0)  433 us
    pallas_call x1, Pallas kernels, symmetric_product(): pl.pallas_call(block_product_kernel, grid_spec=grid_spec, out_shape=jax.S...  131 us
    unnamed x18, local copies, waits for them, and re-layouts  26.6 us
  transfers between devices with their start and end apart: 4, of which 2 were waited for; matrix products, arithmetic and copies ran while one was open for 10% of the time, Pallas kernels for 0%

profile of v12, /device:TPU:0, one launch (start us, length us, event | category | flops | bytes accessed | tf_op | source)
XLA Modules:
  0.0 700.4 jit_solution(5632232927316750690)
XLA Ops:
  7.2 0.5 collective-permute-start
  7.8 5.5 collective-permute-done
  13.2 1.7 copy-done.1
  14.9 2.9 gather_fusion
  17.8 1.8 bitcast_select_fusion
  19.7 432.8 %all-gather.2.cloned.1.call-done = bf16[16,5,512,512]{3,2,1,0:T(8,128)(2,1)} async-done(((bf16[1,5,512,512]{3,2,1,0:T(8,128)(2,1)}), bf16[16,5,512,512]{3,2,1,0:T(8,128)(2,1)}) %all-gather.2.cloned.1.call-update) | async-done | bytes 41943056 | tf_op jit(solution)/shard_map/all_gather | solution.py:59
  452.5 13.7 %constant_dynamic-slice_fusion.1 = bf16[8,4,512,512]{3,2,1,0:T(8,128)(2,1)} fusion(bf16[16,5,512,512]{3,2,1,0:T(8,128)(2,1)} %all-gather.2.cloned.1.call-done, s32[]{:T(128)S(6)} %select_n.204), kind=kLoop, calls=%fused_computation.53 | loop fusion | bytes 33554436 | tf_op jit(solution)/shard_map/slice | solution.py:61
  466.9 0.3 select_reduce_fusion
  467.8 0.5 select_convert_fusion
  468.3 0.6 broadcast_select_fusion.2
  469.0 2.3 broadcast_select_fusion.1
  471.3 0.4 pad_maximum_fusion
  471.7 7.1 %convert_bitcast_fusion = bf16[64,128,6,128]{3,0,1,2:T(8,128)(2,1)} fusion(bf16[6,32,128,128]{3,2,1,0:T(8,128)(2,1)S(1)} %bitcast.45, pred[6,128]{1,0:T(8,128)(4,1)S(1)} %get-tuple-element.20, s32[6,32]{1,0:T(8,128)S(1)} %select_reduce_fusion, pred[6,32]{1,0:T(8,128)(4,1)S(1)} %iota_compare_fusion.2), kind=kOutput, calls=%fused_computation.3 | convolution fusion | flops 412114944 | bytes 18876096 | tf_op jit(solution)/shard_map/ckn,ckbj->nbcj/dot_general | solution.py:27
  478.8 12.4 %copy.47 = bf16[64,128,6,128]{3,2,1,0:T(8,128)(2,1)S(1)} copy(bf16[64,128,6,128]{3,0,1,2:T(8,128)(2,1)} %convert_bitcast_fusion) | data formatting | bytes 25165824 | tf_op jit(solution)/shard_map/reshape | solution.py:28
  491.2 12.2 %copy.58 = bf16[1024,8,6,128]{3,1,2,0:T(8,128)(2,1)} copy(bf16[1024,8,6,128]{3,2,1,0:T(8,128)(2,1)S(1)} %bitcast.43) | data formatting | bytes 25165824
  503.4 3.9 convert_bitcast_fusion.1
  507.3 5.2 copy.37
  512.5 131.3 %shard_map.86 = f32[4096,768]{1,0:T(8,128)} custom-call(s32[128]{0:T(128)} %get-tuple-element.18.src_ref, s32[128]{0:T(128)} %get-tuple-element.17.far_ref, s32[128]{0:T(128)} %get-tuple-element.16.pick_ref, s32[128]{0:T(128)} %get-tuple-element.12.flip_ref, bf16[80,512,512]{2,1,0:T(8,128)(2,1)} %bitcast.42, bf16[32,512,512]{2,1,0:T(8,128)(2,1)} %bitcast.4.swap_ref, ...), custom_call_target="tpu_custom_call" | custom-call | tf_op jit(solution)/shard_map/pallas_call | solution.py:94
  643.8 12.6 %copy.36 = f32[4096,768]{0,1:T(8,128)} copy(f32[4096,768]{1,0:T(8,128)} %shard_map.86) | data formatting | bytes 25165824 | tf_op jit(solution)/shard_map/pallas_call | solution.py:94
  656.4 11.1 %fusion.22 = f32[6,128,128]{2,1,0:T(8,128)S(1)} fusion(bf16[4096,6,128]{2,0,1:T(8,128)(2,1)} %bitcast.47, f32[4096,6,128]{0,2,1:T(8,128)} %bitcast.40), kind=kOutput, calls=%fused_computation.74 | convolution fusion | flops 4831838208 | bytes 19267584 | tf_op jit(solution)/shard_map/nca,ncb->cab/dot_general | solution.py:142
  667.5 0.5 collective-permute-start.2
  668.1 12.0 %multiply_multiply_fusion = f32[4096,6,128]{0,2,1:T(8,128)} fusion(f32[4096,6,128]{0,2,1:T(8,128)} %bitcast.41, f32[6,128]{1,0:T(8,128)S(1)} %get-tuple-element.19, f32[4096,6]{0,1:T(8,128)S(1)} %bitcast.49), kind=kLoop, calls=%fused_computation.2 | loop fusion | flops 9437184 | bytes 25267200 | tf_op jit(solution)/shard_map/mul | solution.py:165
  680.1 12.6 %copy.40 = f32[4096,6,128]{2,0,1:T(8,128)} copy(f32[4096,6,128]{0,2,1:T(8,128)} %multiply_multiply_fusion) | data formatting | bytes 25165824
  692.7 0.8 fusion.5
  (46 shorter events, 1.4 us)
Async XLA Ops:
  7.2 445.3 %all-gather.2.cloned.1.call-start = ((), (), s32[]{:S(2)}) async-start(), calls=%async_computation | async-start | bytes 44564480 | tf_op jit(solution)/shard_map/all_gather | solution.py:59
  7.2 6.0 collective-permute-start
  13.2 1.7 copy-start.1
  19.7 447.3 %copy-start.3 = (s32[6,32]{1,0:T(8,128)S(1)}, s32[6,32]{1,0:T(8,128)}, u32[]{:S(2)}) copy-start(s32[6,32]{1,0:T(8,128)} %param.10) | copy-start | bytes 2308
  19.7 447.3 %copy-start.4 = (s32[64]{0:T(128)S(1)}, s32[64]{0:T(128)}, u32[]{:S(2)}) copy-start(s32[64]{0:T(128)} %param.13) | copy-start | bytes 772
  19.7 447.5 %copy-start.6 = (s32[6]{0:T(128)S(1)}, s32[6]{0:T(128)}, u32[]{:S(2)}) copy-start(s32[6]{0:T(128)} %param.11) | copy-start | bytes 76
  19.7 448.0 %copy-start.5 = (s32[6]{0:T(128)S(1)}, s32[6]{0:T(128)}, u32[]{:S(2)}) copy-start(s32[6]{0:T(128)} %param.12) | copy-start | bytes 76
  19.7 449.3 %copy-start = (bf16[6,2048,128]{2,1,0:T(8,128)(2,1)S(1)}, bf16[6,2048,128]{2,1,0:T(8,128)(2,1)}, u32[]{:S(2)}) copy-start(bf16[6,2048,128]{2,1,0:T(8,128)(2,1)} %param.8) | copy-start | bytes 9437188
  466.2 46.3 %collective-permute-start.1 = (bf16[8,4,512,512]{3,2,1,0:T(8,128)(2,1)}, bf16[8,4,512,512]{3,2,1,0:T(8,128)(2,1)}, u32[]{:S(2)}, u32[]{:S(2)}) collective-permute-start(bf16[8,4,512,512]{3,2,1,0:T(8,128)(2,1)} %constant_dynamic-slice_fusion.1), channel_id=1, source_target_pairs={{0,1},{1,0},{2,3},{3,2},{4,5},{5,4},{6,7},{7,6},{8,9},{9,8},{10,11... | collective-permute-start | bytes 50331656 | tf_op jit(solution)/shard_map/ppermute | solution.py:61
  667.5 25.2 %collective-permute-start.2 = (f32[6,128,128]{2,1,0:T(8,128)S(1)}, f32[6,128,128]{2,1,0:T(8,128)S(1)}, u32[]{:S(2)}, u32[]{:S(2)}) collective-permute-start(f32[6,128,128]{2,1,0:T(8,128)S(1)} %fusion.22), channel_id=1, source_target_pairs={{0,1},{1,0},{2,3},{3,2},{4,5},{5,4},{6,7},{7,6},{8,9},{9,8},{10,11... | collective-permute-start | bytes 1179656 | tf_op jit(solution)/shard_map/ppermute | solution.py:147
  680.1 12.6 %copy-start.2 = (f32[6,64,128]{2,1,0:T(8,128)S(1)}, f32[6,64,128]{2,1,0:T(8,128)}, u32[]{:S(2)}) copy-start(f32[6,64,128]{2,1,0:T(8,128)} %param.9) | copy-start | bytes 589828
Sparse Core Ops, SparseCore 0:
  19.8 432.6 all-gather.1
